TPU v7x, 128 devices: a whole 4x4x4 slice. The times are simulated.
128 devices in a mesh: seq: 16 (over x, z_lo, core), chan: 8 (over y, z_hi).
Axes of the slice: x: 4, y: 4, z: 4 (z_hi: 2, z_lo: 2; z = z_hi * 2 + z_lo), core: 2. Of those that a mesh axis runs over, the one named last changes fastest.
Arguments:
- gate_in: bfloat16 [8192, 2048], P('seq', 'chan'), may hold values from -6 to 6
- out_gate: bfloat16 [8192, 2048], P('seq', 'chan'), may hold values from -6 to 6
- value_in: bfloat16 [8192, 2048], P('seq', 'chan'), may hold values from -6 to 6
- out_grad: bfloat16 [8192, 2048], P('seq', 'chan'), may hold values from -6 to 6
- skip_gain: float32 [2048], P('chan'), may hold values from -1 to 1
- filter_taps: float32 [8192, 256], P('seq'), may hold values from -0.0625 to 0.0625
Outputs:
- grad_gate: bfloat16 [8192, 2048], P('seq', 'chan')
- grad_out_gate: bfloat16 [8192, 2048], P('seq', 'chan')
- grad_value: bfloat16 [8192, 2048], P('seq', 'chan')
- skip_grad: float32 [2048], P('chan')
- taps_grad: float32 [8192, 256], P('seq')
All inputs are finite; a program needn't handle non-finite values.
Results may differ from a plain program's by a relative error of at most 0.0052.
Values sent between devices are 32-bit elements; how exact they have to be, the bound alone decides.
No kernel may reach another device: no remote copies, remote signals or barrier semaphores. Data moves between devices by JAX's collectives and lax.ppermute only.
A program may use at most 128 MiB of HBM per device.

v0:
```python
import math

import jax
import jax.numpy as jnp
from jax import lax
from jax.sharding import PartitionSpec as P

HIGH = lax.Precision.HIGH
F32 = jnp.float32


def trig(a_count, b_count, period, scale=1.0):
    a_ids = lax.iota(jnp.int32, a_count)[:, None]
    b_ids = lax.iota(jnp.int32, b_count)[None, :]
    turns = (a_ids * b_ids) % period
    angle = turns.astype(F32) * (2.0 * math.pi / period)
    return jnp.cos(angle) * scale, jnp.sin(angle) * scale


def mm(spec, a, b):
    return jnp.einsum(spec, a, b, precision=HIGH, preferred_element_type=F32)


def body(gate_in, out_gate, value_in, out_grad, skip_gain, filter_taps):
    seq_n = lax.axis_size("seq")
    chan_n = lax.axis_size("chan")
    rows, local_ch = gate_in.shape
    filters = filter_taps.shape[1]
    dev_n = seq_n * chan_n
    per_dev = local_ch // dev_n
    part = rows // chan_n
    assert local_ch == filters and local_ch % dev_n == 0 and rows % chan_n == 0
    length = 2 * seq_n * rows
    k1 = seq_n + 1
    span = per_dev * rows
    cc = chan_n * per_dev
    pad_w = 128

    mixed_bf = lax.optimization_barrier(
        (gate_in.astype(F32) * value_in.astype(F32)).astype(jnp.bfloat16)
    )
    gated_bf = lax.optimization_barrier(
        (out_grad.astype(F32) * out_gate.astype(F32)).astype(jnp.bfloat16)
    )
    mixed = mixed_bf.astype(F32)
    gated = gated_bf.astype(F32)

    chan_id = lax.axis_index("chan")
    taps_rows = lax.dynamic_slice_in_dim(filter_taps, chan_id * part, part, axis=0)
    send = jnp.concatenate(
        [
            mixed.T.reshape(dev_n, span),
            gated.T.reshape(dev_n, span),
            taps_rows.T.reshape(dev_n, per_dev * part),
        ],
        axis=1,
    )
    recv = lax.all_to_all(send, ("seq", "chan"), 0, 0, tiled=True).reshape(seq_n, chan_n, -1)

    def by_filter(block):
        return block.reshape(seq_n, chan_n, per_dev, rows).transpose(0, 2, 1, 3).reshape(seq_n, cc, rows)

    m_pos = by_filter(recv[:, :, :span])
    g_pos = by_filter(recv[:, :, span : 2 * span])
    h_pos = recv[:, :, 2 * span :].reshape(seq_n, chan_n, per_dev, part)
    h_pos = h_pos.transpose(0, 2, 1, 3).reshape(seq_n, per_dev, rows)
    skip_mine = jnp.sum(m_pos * g_pos, axis=(0, 2)).reshape(per_dev, chan_n).T

    c1, s1 = trig(k1, seq_n, 2 * seq_n)
    tw_c, tw_s = trig(k1, rows, length)
    tw_c = tw_c[:, None, :]
    tw_s = tw_s[:, None, :]
    c2, s2 = trig(rows, rows, rows)
    w_fwd = jnp.concatenate(
        [jnp.concatenate([c2, -s2], axis=1), jnp.concatenate([s2, c2], axis=1)], axis=0
    )
    w_inv = jnp.concatenate(
        [jnp.concatenate([c2, s2], axis=1), jnp.concatenate([-s2, c2], axis=1)], axis=0
    )
    weight = jnp.where(
        (lax.iota(jnp.int32, k1) == 0) | (lax.iota(jnp.int32, k1) == seq_n), 1.0, 2.0
    ) / length
    ci, si = trig(seq_n, k1, 2 * seq_n)
    ci = ci * weight[None, :]
    si = si * weight[None, :]

    fields = jnp.concatenate([m_pos, g_pos, h_pos], axis=1)
    are = mm("ks,scr->kcr", c1, fields)
    aim = mm("ks,scr->kcr", -s1, fields)
    turned = jnp.concatenate([are * tw_c + aim * tw_s, aim * tw_c - are * tw_s], axis=2)
    spec = mm("kcn,nm->kcm", turned, w_fwd)

    mre, mim = spec[:, :cc, :rows], spec[:, :cc, rows:]
    gre, gim = spec[:, cc : 2 * cc, :rows], spec[:, cc : 2 * cc, rows:]
    h = spec[:, 2 * cc :]
    h = jnp.broadcast_to(h[:, :, None, :], (k1, per_dev, chan_n, 2 * rows)).reshape(k1, cc, 2 * rows)
    hre, him = h[:, :, :rows], h[:, :, rows:]

    conv_s = jnp.concatenate([hre * mre - him * mim, hre * mim + him * mre], axis=2)
    corr_s = jnp.concatenate([gre * hre + gim * him, gim * hre - gre * him], axis=2)
    taps_s = jnp.concatenate([gre * mre + gim * mim, gim * mre - gre * mim], axis=2)
    taps_s = jnp.sum(taps_s.reshape(k1, per_dev, chan_n, 2 * rows), axis=2)

    prod = jnp.concatenate([conv_s, corr_s, taps_s], axis=1)
    z = mm("kcn,nm->kcm", prod, w_inv)
    zre, zim = z[:, :, :rows], z[:, :, rows:]
    ure = zre * tw_c - zim * tw_s
    uim = zre * tw_s + zim * tw_c
    y = mm("ik,kcr->icr", ci, ure) - mm("ik,kcr->icr", si, uim)

    def by_copy(block):
        return block.reshape(seq_n, per_dev, chan_n, rows).transpose(0, 2, 1, 3).reshape(seq_n, chan_n, span)

    conv_blk = by_copy(y[:, :cc])
    corr_blk = by_copy(y[:, cc : 2 * cc])
    taps_blk = jnp.broadcast_to(y[:, 2 * cc :].reshape(seq_n, 1, span), (seq_n, chan_n, span))
    skip_blk = jnp.broadcast_to(
        jnp.pad(skip_mine, ((0, 0), (0, pad_w - per_dev)))[None], (seq_n, chan_n, pad_w)
    )
    out_send = jnp.concatenate([conv_blk, corr_blk, taps_blk, skip_blk], axis=2)
    back = lax.all_to_all(out_send.reshape(dev_n, -1), ("seq", "chan"), 0, 0, tiled=True)
    conv_out = back[:, :span].reshape(local_ch, rows).T
    corr_out = back[:, span : 2 * span].reshape(local_ch, rows).T
    taps_grad = back[:, 2 * span : 3 * span].reshape(filters, rows).T
    skip_grad = back[:, 3 * span : 3 * span + per_dev].reshape(local_ch)

    out_f32 = out_grad.astype(F32)
    grad_out_gate = (out_f32 * (conv_out + skip_gain[None] * mixed)).astype(jnp.bfloat16)
    mix_grad = corr_out + skip_gain[None] * gated
    grad_gate = (mix_grad * value_in.astype(F32)).astype(jnp.bfloat16)
    grad_value = (mix_grad * gate_in.astype(F32)).astype(jnp.bfloat16)
    return (grad_gate, grad_out_gate, grad_value, skip_grad, taps_grad)


def solution(mesh):
    placed = (
        P("seq", "chan"),
        P("seq", "chan"),
        P("seq", "chan"),
        P("seq", "chan"),
        P("chan"),
        P("seq", None),
    )
    return jax.shard_map(
        body,
        mesh=mesh,
        in_specs=placed,
        out_specs=(P("seq", "chan"), P("seq", "chan"), P("seq", "chan"), P("chan"), P("seq", None)),
        check_vma=False,
    )
```

profile of v0, /device:TPU:1, one launch (start us, length us, event | category | flops | bytes accessed | tf_op | source)
XLA Modules:
  0.0 104.1 jit_solution(10577063126875586772)
XLA Ops:
  0.7 1.0 copy-done
  1.9 1.1 %copy.32 = bf16[512,256]{0,1:T(8,128)(2,1)S(1)} copy(bf16[512,256]{1,0:T(8,128)(2,1)} %param.6) | data formatting | bytes 524288 | tf_op args[0]
  3.0 1.1 %copy.33 = bf16[512,256]{0,1:T(8,128)(2,1)S(1)} copy(bf16[512,256]{1,0:T(8,128)(2,1)} %param.8) | data formatting | bytes 524288 | tf_op args[2]
  5.1 2.2 %copy.37 = f32[128,1,2176]{2,1,0:T(1,128)} copy(f32[128,1,2176]{2,0,1:T(8,128)S(1)} %maximum_bitcast_fusion.1) | data formatting | bytes 2228224 | tf_op jit(solution)/shard_map/all_to_all | solution.py:58
  7.2 11.5 %all-to-all-start = ((f32[128,1,2176]{2,1,0:T(1,128)}), f32[128,1,2176]{2,1,0:T(1,128)S(1)}, u32[]{:S(2)}, u32[]{:S(2)}) async-start(f32[128,1,2176]{2,1,0:T(1,128)} %copy.37), calls=%async_computation | async-start | bytes 2228224 | tf_op jit(solution)/shard_map/all_to_all | solution.py:58
  19.0 4.6 %fusion.51 = f32[512,512]{1,0:T(8,128)} fusion(), kind=kLoop, calls=%fused_computation.83 | loop fusion | flops 3932160 | bytes 1048576 | tf_op jit(solution)/shard_map/neg | solution.py:75
  23.6 5.0 %fusion.49 = (f32[512,512]{1,0:T(8,128)}, f32[512,512]{1,0:T(8,128)}) fusion(), kind=kLoop, calls=%fused_computation.81 | loop fusion | flops 3670016 | bytes 2097152 | tf_op jit(solution)/shard_map/sin | solution.py:17
  28.5 10.4 %all-to-all-done = f32[128,1,2176]{2,1,0:T(1,128)S(1)} async-done(((f32[128,1,2176]{2,1,0:T(1,128)}), f32[128,1,2176]{2,1,0:T(1,128)S(1)}, u32[]{:S(2)}, u32[]{:S(2)}) %all-to-all-start) | async-done | bytes 1114144 | tf_op jit(solution)/shard_map/all_to_all | solution.py:58
  39.0 0.6 slice.78
  39.7 0.4 reshape.135
  40.2 1.0 reshape.139
  41.2 0.7 reshape.140
  41.9 0.4 reshape.137
  43.4 0.9 fusion.41
  44.4 1.3 %multiply_add_fusion = (f32[17,34,512]{2,0,1:T(8,128)S(1)}, f32[17,34,512]{2,0,1:T(8,128)S(1)}) fusion(f32[17,34,512]{2,0,1:T(8,128)S(1)} %fusion.41, f32[17,512]{1,0:T(8,128)S(1)} %get-tuple-element.33, f32[17,512]{1,0:T(8,128)S(1)} %get-tuple-element.34, f32[16,2,512]{2,0,1:T(8,128)S(1)} %copy-done.4, f32[16,16,512]{2,0,1:T(8,128)S(1)} %bitcast.88, ...), kind=kOutput, calls=%fused_computation.27 | convolution fusion | flops 30746608 | bytes 4734976 | tf_op jit(solution)/shard_map/ks,scr->kcr/dot_general | solution.py:21
  46.1 0.8 copy-done.1
  47.5 5.7 %fusion.2 = f32[17,34,1024]{2,1,0:T(8,128)S(1)} fusion(f32[512,512]{1,0:T(8,128)S(1)} %copy-done.3, f32[512,512]{1,0:T(8,128)S(1)} %copy-done.2, f32[512,512]{1,0:T(8,128)S(1)} %copy-done.1, f32[17,34,1024]{2,0,1:T(8,128)S(1)} %pad_maximum_fusion.6), kind=kOutput, calls=%fused_computation.6 | convolution fusion | flops 3639607296 | bytes 7880704 | tf_op jit(solution)/shard_map/kcn,nm->kcm/dot_general | solution.py:21
  54.6 6.8 %fusion.6 = f32[17,34,1024]{2,0,1:T(8,128)S(1)} fusion(f32[512,512]{1,0:T(8,128)S(1)} %copy-done.3, f32[512,512]{1,0:T(8,128)S(1)} %copy-done.1, f32[512,512]{1,0:T(8,128)S(1)} %copy-done.2, f32[17,34,1024]{2,1,0:T(8,128)S(1)} %pad_maximum_fusion.7), kind=kOutput, calls=%fused_computation.9 | convolution fusion | flops 3639607296 | bytes 7880704 | tf_op jit(solution)/shard_map/kcn,nm->kcm/dot_general | solution.py:21
  61.4 0.8 fusion.14
  62.2 0.8 fusion.26
  63.1 0.4 copy.70
  63.7 0.4 copy.69
  64.4 1.7 %copy.47 = f32[128,1,3200]{2,1,0:T(1,128)S(1)} copy(f32[128,1,3200]{2,0,1:T(8,128)S(1)} %maximum_bitcast_fusion) | data formatting | bytes 3276800 | tf_op jit(solution)/shard_map/all_to_all | solution.py:121
  66.1 29.4 %all_to_all.21 = f32[128,1,3200]{2,1,0:T(1,128)S(1)} all-to-all(f32[128,1,3200]{2,1,0:T(1,128)S(1)} %copy.47), channel_id=1, replica_groups=mesh['seq'=16,'chan'=8] {'seq','chan'}, dimensions={0} | all-to-all | bytes 3276800 | tf_op jit(solution)/shard_map/all_to_all | solution.py:121
  95.5 1.0 fusion.110
  96.6 0.7 reshape.147
  97.3 1.1 %reshape.148 = f32[256,512]{1,0:T(8,128)S(1)} reshape(f32[128,1024]{1,0:T(8,128)} %get-tuple-element.23) | data formatting | bytes 1048576 | tf_op jit(solution)/shard_map/reshape | solution.py:124
  98.4 1.0 copy.51
  99.6 1.0 fusion.42
  100.6 1.8 %copy.50 = bf16[512,256]{1,0:T(8,128)(2,1)} copy(bf16[512,256]{0,1:T(8,128)(2,1)} %get-tuple-element.30) | data formatting | bytes 524288
  102.4 0.8 copy.48
  103.2 0.8 copy.49
  (54 shorter events, 5.7 us)
Async XLA Ops:
  0.6 1.0 %copy-start = (f32[512,256]{1,0:T(8,128)S(1)}, f32[512,256]{1,0:T(8,128)}, u32[]{:S(2)}) copy-start(f32[512,256]{1,0:T(8,128)} %param.11) | copy-start | bytes 1572868
  0.6 3.4 %copy-start.5 = (bf16[512,256]{1,0:T(8,128)(2,1)S(1)}, bf16[512,256]{1,0:T(8,128)(2,1)}, u32[]{:S(2)}) copy-start(bf16[512,256]{1,0:T(8,128)(2,1)} %param.9) | copy-start | bytes 786436
  0.7 3.6 %copy-start.6 = (bf16[512,256]{1,0:T(8,128)(2,1)S(1)}, bf16[512,256]{1,0:T(8,128)(2,1)}, u32[]{:S(2)}) copy-start(bf16[512,256]{1,0:T(8,128)(2,1)} %param.7) | copy-start | bytes 786436
  7.2 31.7 %all-to-all-start = ((f32[128,1,2176]{2,1,0:T(1,128)}), f32[128,1,2176]{2,1,0:T(1,128)S(1)}, u32[]{:S(2)}, u32[]{:S(2)}) async-start(f32[128,1,2176]{2,1,0:T(1,128)} %copy.37), calls=%async_computation | async-start | bytes 2228224 | tf_op jit(solution)/shard_map/all_to_all | solution.py:58
  42.4 1.0 %copy-start.4 = (f32[16,2,512]{2,0,1:T(8,128)S(1)}, f32[16,2,512]{2,0,1:T(8,128)}, u32[]{:S(2)}) copy-start(f32[16,2,512]{2,0,1:T(8,128)} %reshape.140) | copy-start | bytes 196612
  45.6 1.2 %copy-start.1 = (f32[512,512]{1,0:T(8,128)S(1)}, f32[512,512]{1,0:T(8,128)}, u32[]{:S(2)}) copy-start(f32[512,512]{1,0:T(8,128)} %fusion.51) | copy-start | bytes 3145732
  45.6 1.5 %copy-start.2 = (f32[512,512]{1,0:T(8,128)S(1)}, f32[512,512]{1,0:T(8,128)}, u32[]{:S(2)}) copy-start(f32[512,512]{1,0:T(8,128)} %get-tuple-element.35) | copy-start | bytes 3145732
  45.7 1.8 %copy-start.3 = (f32[512,512]{1,0:T(8,128)S(1)}, f32[512,512]{1,0:T(8,128)}, u32[]{:S(2)}) copy-start(f32[512,512]{1,0:T(8,128)} %get-tuple-element.36) | copy-start | bytes 3145732
  98.4 1.2 %copy-start.7 = (f32[256]{0:T(256)S(1)}, f32[256]{0:T(256)}, u32[]{:S(2)}) copy-start(f32[256]{0:T(256)} %param.10) | copy-start | bytes 3076
where the time goes:
time: 104 us
  blocking collectives  29.4 us (28%)
  local copies, waits for them, and re-layouts  22.2 us (21%)
  matrix products  16.3 us (16%)
  other arithmetic  13.2 us (13%)
  starting transfers between devices  11.5 us (11%)
  waiting for transfers between devices  10.4 us (10%)
  between operations  1.1 us (1%)
    all_to_all x1, blocking collectives, body(): lax.all_to_all(out_send.reshape(dev_n, -1), ('seq', 'chan'), 0, 0, tiled=...  29.4 us
    dot_general x6, matrix products, mm(): return jnp.einsum(spec, a, b, precision=HIGH, preferred_element_type=F32)  16.3 us
    all_to_all x1, starting transfers between devices, body(): lax.all_to_all(send, ('seq', 'chan'), 0, 0, tiled=True)  11.5 us
    all_to_all x1, waiting for transfers between devices, body(): lax.all_to_all(send, ('seq', 'chan'), 0, 0, tiled=True)  10.4 us
    unnamed x29, local copies, waits for them, and re-layouts  9.79 us
    sin x2, other arithmetic, trig(): return (jnp.cos(angle) * scale, jnp.sin(angle) * scale)  5.18 us
    neg x1, other arithmetic, body(): -s2  4.62 us
    all_to_all x1, local copies, waits for them, and re-layouts, body(): lax.all_to_all(send, ('seq', 'chan'), 0, 0, tiled=True)  2.15 us
  transfers between devices with their start and end apart: 1, of which 1 were waited for; matrix products, arithmetic and copies ran while one was open for 9% of the time, Pallas kernels for 0%

commit v1 on v0

--- a/solution.py
+++ b/solution.py
@@ -47,14 +47,11 @@
 
     chan_id = lax.axis_index("chan")
     taps_rows = lax.dynamic_slice_in_dim(filter_taps, chan_id * part, part, axis=0)
-    send = jnp.concatenate(
-        [
-            mixed.T.reshape(dev_n, span),
-            gated.T.reshape(dev_n, span),
-            taps_rows.T.reshape(dev_n, per_dev * part),
-        ],
-        axis=1,
-    )
+    def by_target(block):
+        width = block.shape[0]
+        return block.T.reshape(per_dev, dev_n, width).transpose(1, 0, 2).reshape(dev_n, per_dev * width)
+
+    send = jnp.concatenate([by_target(mixed), by_target(gated), by_target(taps_rows)], axis=1)
     recv = lax.all_to_all(send, ("seq", "chan"), 0, 0, tiled=True).reshape(seq_n, chan_n, -1)
 
     def by_filter(block):
@@ -119,10 +116,15 @@
     )
     out_send = jnp.concatenate([conv_blk, corr_blk, taps_blk, skip_blk], axis=2)
     back = lax.all_to_all(out_send.reshape(dev_n, -1), ("seq", "chan"), 0, 0, tiled=True)
-    conv_out = back[:, :span].reshape(local_ch, rows).T
-    corr_out = back[:, span : 2 * span].reshape(local_ch, rows).T
-    taps_grad = back[:, 2 * span : 3 * span].reshape(filters, rows).T
-    skip_grad = back[:, 3 * span : 3 * span + per_dev].reshape(local_ch)
+    def by_channel(start):
+        return jnp.concatenate(
+            [back[:, start + f2 * rows : start + (f2 + 1) * rows].T for f2 in range(per_dev)], axis=1
+        )
+
+    conv_out = by_channel(0)
+    corr_out = by_channel(span)
+    taps_grad = by_channel(2 * span)
+    skip_grad = back[:, 3 * span : 3 * span + per_dev].T.reshape(local_ch)
 
     out_f32 = out_grad.astype(F32)
     grad_out_gate = (out_f32 * (conv_out + skip_gain[None] * mixed)).astype(jnp.bfloat16)

time: 104 us -> 107 us (1.029)
  other arithmetic: 13.2 us -> 15.3 us
    transpose x2 -> x7, local copies, waits for them, and re-layouts: 0.1 us -> 2.85 us  [the longest x4 1.2 us: by_target(): block.T.reshape(per_dev, dev_n, width).transpose(1, 0, 2)]
    reshape x7 -> x1, local copies, waits for them, and re-layouts: 2.42 us -> 0.04 us  [by_target(): block.T.reshape(per_dev, dev_n, width).transpose(1, 0, 2)]
    unnamed x29 -> x27, local copies, waits for them, and re-layouts: 9.79 us -> 10.7 us
where the time goes in v1:
time: 107 us
  blocking collectives  29.4 us (27%)
  local copies, waits for them, and re-layouts  22.8 us (21%)
  matrix products  16.3 us (15%)
  other arithmetic  15.3 us (14%)
  starting transfers between devices  11.5 us (11%)
  waiting for transfers between devices  10.4 us (10%)
    all_to_all x1, blocking collectives, body(): lax.all_to_all(out_send.reshape(dev_n, -1), ('seq', 'chan'), 0, 0, tiled=...  29.4 us
    dot_general x6, matrix products, mm(): return jnp.einsum(spec, a, b, precision=HIGH, preferred_element_type=F32)  16.3 us
    all_to_all x1, starting transfers between devices, body(): lax.all_to_all(send, ('seq', 'chan'), 0, 0, tiled=True)  11.5 us
    unnamed x27, local copies, waits for them, and re-layouts  10.7 us
    all_to_all x1, waiting for transfers between devices, body(): lax.all_to_all(send, ('seq', 'chan'), 0, 0, tiled=True)  10.4 us
    sin x2, other arithmetic, trig(): return (jnp.cos(angle) * scale, jnp.sin(angle) * scale)  5.16 us
    neg x1, other arithmetic, body(): -s2  4.62 us
    all_to_all x1, local copies, waits for them, and re-layouts, body(): lax.all_to_all(send, ('seq', 'chan'), 0, 0, tiled=True)  2.36 us
  transfers between devices with their start and end apart: 1, of which 1 were waited for; matrix products, arithmetic and copies ran while one was open for 9% of the time, Pallas kernels for 0%

profile of v1, /device:TPU:1, one launch (start us, length us, event | category | flops | bytes accessed | tf_op | source)
XLA Modules:
  0.0 106.6 jit_solution(7804952826168672047)
XLA Ops:
  0.7 1.0 copy-done
  1.7 1.1 %copy.58 = bf16[512,256]{0,1:T(8,128)(2,1)S(1)} copy(bf16[512,256]{1,0:T(8,128)(2,1)} %param.6) | data formatting | bytes 524288 | tf_op args[0]
  2.8 1.1 %copy.59 = bf16[512,256]{0,1:T(8,128)(2,1)S(1)} copy(bf16[512,256]{1,0:T(8,128)(2,1)} %param.8) | data formatting | bytes 524288 | tf_op args[2]
  3.9 1.1 %copy.61 = bf16[512,256]{0,1:T(8,128)(2,1)S(1)} copy(bf16[512,256]{1,0:T(8,128)(2,1)} %param.9) | data formatting | bytes 524288 | tf_op args[3]
  5.7 1.0 copy.60
  6.7 1.1 %maximum_bitcast_fusion.1 = f32[128,1,2176]{0,2,1:T(8,128)S(1)} fusion(f32[128,128]{0,1:T(8,128)S(1)} %bitcast.123, f32[128,1024]{0,1:T(8,128)S(1)} %bitcast.114, f32[128,1024]{0,1:T(8,128)} %bitcast.115), kind=kLoop, calls=%fused_computation.38 | loop fusion | flops 557056 | bytes 2228224 | tf_op jit(solution)/shard_map/all_to_all | solution.py:55
  7.8 2.4 %copy.65 = f32[128,1,2176]{2,1,0:T(1,128)} copy(f32[128,1,2176]{0,2,1:T(8,128)S(1)} %maximum_bitcast_fusion.1) | data formatting | bytes 2228224 | tf_op jit(solution)/shard_map/all_to_all | solution.py:55
  10.1 11.5 %all-to-all-start = ((f32[128,1,2176]{2,1,0:T(1,128)}), f32[128,1,2176]{2,1,0:T(1,128)S(1)}, u32[]{:S(2)}, u32[]{:S(2)}) async-start(f32[128,1,2176]{2,1,0:T(1,128)} %copy.65), calls=%async_computation | async-start | bytes 2228224 | tf_op jit(solution)/shard_map/all_to_all | solution.py:55
  21.9 4.6 %fusion.49 = f32[512,512]{1,0:T(8,128)} fusion(), kind=kLoop, calls=%fused_computation.80 | loop fusion | flops 3932160 | bytes 1048576 | tf_op jit(solution)/shard_map/neg | solution.py:72
  26.5 5.0 %fusion.47 = (f32[512,512]{1,0:T(8,128)}, f32[512,512]{1,0:T(8,128)}) fusion(), kind=kLoop, calls=%fused_computation.78 | loop fusion | flops 3670016 | bytes 2097152 | tf_op jit(solution)/shard_map/sin | solution.py:17
  31.4 10.4 %all-to-all-done = f32[128,1,2176]{2,1,0:T(1,128)S(1)} async-done(((f32[128,1,2176]{2,1,0:T(1,128)}), f32[128,1,2176]{2,1,0:T(1,128)S(1)}, u32[]{:S(2)}, u32[]{:S(2)}) %all-to-all-start) | async-done | bytes 1114144 | tf_op jit(solution)/shard_map/all_to_all | solution.py:55
  41.9 0.6 slice.90
  42.6 0.4 reshape.138
  43.1 1.0 reshape.142
  44.1 0.7 reshape.143
  46.3 0.9 fusion.41
  47.2 1.3 %multiply_add_fusion = (f32[17,34,512]{2,0,1:T(8,128)S(1)}, f32[17,34,512]{2,0,1:T(8,128)S(1)}) fusion(f32[17,34,512]{2,0,1:T(8,128)S(1)} %fusion.41, f32[17,512]{1,0:T(8,128)S(1)} %get-tuple-element.41, f32[17,512]{1,0:T(8,128)S(1)} %get-tuple-element.42, f32[16,2,512]{2,0,1:T(8,128)S(1)} %copy-done.4, f32[16,16,512]{2,0,1:T(8,128)S(1)} %bitcast.106, ...), kind=kOutput, calls=%fused_computation.27 | convolution fusion | flops 30746608 | bytes 4734976 | tf_op jit(solution)/shard_map/ks,scr->kcr/dot_general | solution.py:21
  49.0 0.8 copy-done.1
  50.4 5.7 %fusion.2 = f32[17,34,1024]{2,1,0:T(8,128)S(1)} fusion(f32[512,512]{1,0:T(8,128)S(1)} %copy-done.3, f32[512,512]{1,0:T(8,128)S(1)} %copy-done.2, f32[512,512]{1,0:T(8,128)S(1)} %copy-done.1, f32[17,34,1024]{2,0,1:T(8,128)S(1)} %pad_maximum_fusion.6), kind=kOutput, calls=%fused_computation.6 | convolution fusion | flops 3639607296 | bytes 7880704 | tf_op jit(solution)/shard_map/kcn,nm->kcm/dot_general | solution.py:21
  57.5 6.8 %fusion.6 = f32[17,34,1024]{2,0,1:T(8,128)S(1)} fusion(f32[512,512]{1,0:T(8,128)S(1)} %copy-done.3, f32[512,512]{1,0:T(8,128)S(1)} %copy-done.1, f32[512,512]{1,0:T(8,128)S(1)} %copy-done.2, f32[17,34,1024]{2,1,0:T(8,128)S(1)} %pad_maximum_fusion.7), kind=kOutput, calls=%fused_computation.9 | convolution fusion | flops 3639607296 | bytes 7880704 | tf_op jit(solution)/shard_map/kcn,nm->kcm/dot_general | solution.py:21
  64.3 0.8 fusion.14
  65.1 0.8 fusion.26
  67.3 1.7 %copy.75 = f32[128,1,3200]{2,1,0:T(1,128)S(1)} copy(f32[128,1,3200]{2,0,1:T(8,128)S(1)} %maximum_bitcast_fusion) | data formatting | bytes 3276800 | tf_op jit(solution)/shard_map/all_to_all | solution.py:118
  68.9 29.4 %all_to_all.21 = f32[128,1,3200]{2,1,0:T(1,128)S(1)} all-to-all(f32[128,1,3200]{2,1,0:T(1,128)S(1)} %copy.75), channel_id=1, replica_groups=mesh['seq'=16,'chan'=8] {'seq','chan'}, dimensions={0} | all-to-all | bytes 3276800 | tf_op jit(solution)/shard_map/all_to_all | solution.py:118
  98.5 1.0 slice_bitcast_fusion.1
  99.5 0.6 copy.76
  100.1 1.0 fusion.42
  101.1 1.8 %copy.79 = bf16[512,256]{1,0:T(8,128)(2,1)} copy(bf16[512,256]{0,1:T(8,128)(2,1)} %get-tuple-element.38) | data formatting | bytes 524288
  102.9 1.1 pad_maximum_fusion.11
  104.0 1.0 copy.80
  105.0 0.8 copy.77
  105.8 0.8 copy.78
  (50 shorter events, 6.3 us)
Async XLA Ops:
  0.6 1.0 copy-start
  0.6 4.5 %copy-start.5 = (bf16[512,256]{1,0:T(8,128)(2,1)S(1)}, bf16[512,256]{1,0:T(8,128)(2,1)}, u32[]{:S(2)}) copy-start(bf16[512,256]{1,0:T(8,128)(2,1)} %param.7) | copy-start | bytes 786436
  10.1 31.7 %all-to-all-start = ((f32[128,1,2176]{2,1,0:T(1,128)}), f32[128,1,2176]{2,1,0:T(1,128)S(1)}, u32[]{:S(2)}, u32[]{:S(2)}) async-start(f32[128,1,2176]{2,1,0:T(1,128)} %copy.65), calls=%async_computation | async-start | bytes 2228224 | tf_op jit(solution)/shard_map/all_to_all | solution.py:55
  45.2 1.0 copy-start.4
  48.5 1.2 %copy-start.1 = (f32[512,512]{1,0:T(8,128)S(1)}, f32[512,512]{1,0:T(8,128)}, u32[]{:S(2)}) copy-start(f32[512,512]{1,0:T(8,128)} %fusion.49) | copy-start | bytes 3145732
  48.5 1.5 %copy-start.2 = (f32[512,512]{1,0:T(8,128)S(1)}, f32[512,512]{1,0:T(8,128)}, u32[]{:S(2)}) copy-start(f32[512,512]{1,0:T(8,128)} %get-tuple-element.43) | copy-start | bytes 3145732
  48.5 1.8 %copy-start.3 = (f32[512,512]{1,0:T(8,128)S(1)}, f32[512,512]{1,0:T(8,128)}, u32[]{:S(2)}) copy-start(f32[512,512]{1,0:T(8,128)} %get-tuple-element.44) | copy-start | bytes 3145732
  98.4 1.7 %copy-start.6 = (f32[256]{0:T(256)S(1)}, f32[256]{0:T(256)}, u32[]{:S(2)}) copy-start(f32[256]{0:T(256)} %param.10) | copy-start | bytes 3076

commit v2 on v1

--- a/solution.py
+++ b/solution.py
@@ -3,6 +3,8 @@
 import jax
 import jax.numpy as jnp
 from jax import lax
+from jax.experimental import pallas as pl
+from jax.experimental.pallas import tpu as pltpu
 from jax.sharding import PartitionSpec as P
 
 HIGH = lax.Precision.HIGH
@@ -36,22 +38,24 @@
     cc = chan_n * per_dev
     pad_w = 128
 
-    mixed_bf = lax.optimization_barrier(
-        (gate_in.astype(F32) * value_in.astype(F32)).astype(jnp.bfloat16)
-    )
-    gated_bf = lax.optimization_barrier(
-        (out_grad.astype(F32) * out_gate.astype(F32)).astype(jnp.bfloat16)
-    )
-    mixed = mixed_bf.astype(F32)
-    gated = gated_bf.astype(F32)
-
     chan_id = lax.axis_index("chan")
     taps_rows = lax.dynamic_slice_in_dim(filter_taps, chan_id * part, part, axis=0)
-    def by_target(block):
-        width = block.shape[0]
-        return block.T.reshape(per_dev, dev_n, width).transpose(1, 0, 2).reshape(dev_n, per_dev * width)
+    taps_send = taps_rows.T.reshape(per_dev, dev_n, part).transpose(1, 0, 2).reshape(dev_n, per_dev * part)
 
-    send = jnp.concatenate([by_target(mixed), by_target(gated), by_target(taps_rows)], axis=1)
+    def prep_kernel(gi, vi, og, ot, tr, send):
+        for f2 in range(per_dev):
+            lanes = pl.ds(f2 * dev_n, dev_n)
+            m = (gi[:, lanes].astype(F32) * vi[:, lanes].astype(F32)).astype(jnp.bfloat16).astype(F32)
+            g = (og[:, lanes].astype(F32) * ot[:, lanes].astype(F32)).astype(jnp.bfloat16).astype(F32)
+            send[:, pl.ds(f2 * rows, rows)] = m.T
+            send[:, pl.ds(span + f2 * rows, rows)] = g.T
+        send[:, pl.ds(2 * span, per_dev * part)] = tr[...]
+
+    send = pl.pallas_call(
+        prep_kernel,
+        out_shape=jax.ShapeDtypeStruct((dev_n, 2 * span + per_dev * part), F32),
+        cost_estimate=pl.CostEstimate(flops=4 * rows * local_ch, transcendentals=0, bytes_accessed=4 * 2 * rows * local_ch * 2),
+    )(gate_in, value_in, out_grad, out_gate, taps_send)
     recv = lax.all_to_all(send, ("seq", "chan"), 0, 0, tiled=True).reshape(seq_n, chan_n, -1)
 
     def by_filter(block):
@@ -116,21 +120,37 @@
     )
     out_send = jnp.concatenate([conv_blk, corr_blk, taps_blk, skip_blk], axis=2)
     back = lax.all_to_all(out_send.reshape(dev_n, -1), ("seq", "chan"), 0, 0, tiled=True)
-    def by_channel(start):
-        return jnp.concatenate(
-            [back[:, start + f2 * rows : start + (f2 + 1) * rows].T for f2 in range(per_dev)], axis=1
-        )
+    def tail_kernel(bk, gi, vi, og, ot, sg, o_gg, o_gog, o_gv, o_taps, o_skip):
+        for f2 in range(per_dev):
+            lanes = pl.ds(f2 * dev_n, dev_n)
+            conv = bk[:, pl.ds(f2 * rows, rows)].T
+            corr = bk[:, pl.ds(span + f2 * rows, rows)].T
+            o_taps[:, lanes] = bk[:, pl.ds(2 * span + f2 * rows, rows)].T
+            gate = gi[:, lanes].astype(F32)
+            val = vi[:, lanes].astype(F32)
+            outg = og[:, lanes].astype(F32)
+            m = (gate * val).astype(jnp.bfloat16).astype(F32)
+            g = (outg * ot[:, lanes].astype(F32)).astype(jnp.bfloat16).astype(F32)
+            s = sg[:, lanes]
+            o_gog[:, lanes] = (outg * (conv + s * m)).astype(jnp.bfloat16)
+            mix = corr + s * g
+            o_gg[:, lanes] = (mix * val).astype(jnp.bfloat16)
+            o_gv[:, lanes] = (mix * gate).astype(jnp.bfloat16)
+        o_skip[...] = bk[:, pl.ds(3 * span, pad_w)].T[:per_dev, :]
 
-    conv_out = by_channel(0)
-    corr_out = by_channel(span)
-    taps_grad = by_channel(2 * span)
-    skip_grad = back[:, 3 * span : 3 * span + per_dev].T.reshape(local_ch)
-
-    out_f32 = out_grad.astype(F32)
-    grad_out_gate = (out_f32 * (conv_out + skip_gain[None] * mixed)).astype(jnp.bfloat16)
-    mix_grad = corr_out + skip_gain[None] * gated
-    grad_gate = (mix_grad * value_in.astype(F32)).astype(jnp.bfloat16)
-    grad_value = (mix_grad * gate_in.astype(F32)).astype(jnp.bfloat16)
+    grad_shape = jax.ShapeDtypeStruct((rows, local_ch), jnp.bfloat16)
+    grad_gate, grad_out_gate, grad_value, taps_grad, skip_two = pl.pallas_call(
+        tail_kernel,
+        out_shape=(
+            grad_shape,
+            grad_shape,
+            grad_shape,
+            jax.ShapeDtypeStruct((rows, filters), F32),
+            jax.ShapeDtypeStruct((per_dev, dev_n), F32),
+        ),
+        cost_estimate=pl.CostEstimate(flops=12 * rows * local_ch, transcendentals=0, bytes_accessed=4 * 4 * rows * local_ch * 2),
+    )(back, gate_in, value_in, out_grad, out_gate, skip_gain.reshape(1, local_ch))
+    skip_grad = skip_two.reshape(local_ch)
     return (grad_gate, grad_out_gate, grad_value, skip_grad, taps_grad)
 
 

time: 107 us -> 98 us (0.916)
  local copies, waits for them, and re-layouts: 22.8 us -> 11.8 us
  Pallas kernels: 0 us -> 5.53 us
  other arithmetic: 15.3 us -> 11.2 us
    unnamed x27 -> x11, local copies, waits for them, and re-layouts: 10.7 us -> 3.76 us
    pallas_call x0 -> x2, Pallas kernels: none -> 5.53 us  [the longest x1 3.1 us: body(): pl.pallas_call(tail_kernel, out_shape=(grad_shape, grad_shape, grad_shape...]
    transpose x7 -> x4, local copies, waits for them, and re-layouts: 2.85 us -> 0.63 us  [the longest x2 0.62 us: by_copy(): block.reshape(seq_n, per_dev, chan_n, rows).transpose(0, 2, 1, 3)]
    convert_element_type x5 -> x0, other arithmetic: 1.24 us -> none  [the longest x1 1 us: body(): grad_value = (mix_grad * gate_in.astype(F32)).astype(jnp.bfloat16)]
    all_to_all x2 -> x0, other arithmetic: 1.22 us -> none  [the longest x1 1.11 us: body(): lax.all_to_all(send, ('seq', 'chan'), 0, 0, tiled=True)]
where the time goes in v2:
time: 98 us; the launch traced here: 97.6 us
  blocking collectives  29.4 us (30%)
  matrix products  16.2 us (17%)
  local copies, waits for them, and re-layouts  11.8 us (12%)
  starting transfers between devices  11.5 us (12%)
  other arithmetic  11.2 us (11%)
  waiting for transfers between devices  11.1 us (11%)
  Pallas kernels  5.53 us (6%)
    all_to_all x1, blocking collectives, body(): lax.all_to_all(out_send.reshape(dev_n, -1), ('seq', 'chan'), 0, 0, tiled=...  29.4 us
    dot_general x6, matrix products, mm(): return jnp.einsum(spec, a, b, precision=HIGH, preferred_element_type=F32)  16.2 us
    all_to_all x1, starting transfers between devices, body(): lax.all_to_all(send, ('seq', 'chan'), 0, 0, tiled=True)  11.5 us
    all_to_all x1, waiting for transfers between devices, body(): lax.all_to_all(send, ('seq', 'chan'), 0, 0, tiled=True)  11.1 us
    sin x2, other arithmetic, trig(): return (jnp.cos(angle) * scale, jnp.sin(angle) * scale)  5.18 us
    neg x1, other arithmetic, body(): -s2  3.85 us
    unnamed x11, local copies, waits for them, and re-layouts  3.76 us
    all_to_all x1, local copies, waits for them, and re-layouts, body(): lax.all_to_all(send, ('seq', 'chan'), 0, 0, tiled=True)  3.38 us
  transfers between devices with their start and end apart: 1, of which 1 were waited for; matrix products, arithmetic and copies ran while one was open for 9% of the time, Pallas kernels for 0%

profile of v2, /device:TPU:1, one launch (start us, length us, event | category | flops | bytes accessed | tf_op | source)
XLA Modules:
  0.0 97.6 jit_solution(49911670700013447)
XLA Ops:
  0.7 1.0 %copy-done = f32[512,256]{1,0:T(8,128)S(1)} copy-done((f32[512,256]{1,0:T(8,128)S(1)}, f32[512,256]{1,0:T(8,128)}, u32[]{:S(2)}) %copy-start) | copy-done | bytes 524312
  1.7 0.7 copy.52.tr
  2.5 2.4 %shard_map.101 = f32[128,2176]{1,0:T(8,128)} custom-call(bf16[512,256]{1,0:T(8,128)(2,1)} %gi.3, bf16[512,256]{1,0:T(8,128)(2,1)} %vi.3, bf16[512,256]{1,0:T(8,128)(2,1)} %og.3, bf16[512,256]{1,0:T(8,128)(2,1)} %ot.3, f32[128,128]{1,0:T(8,128)} %copy.52.tr), custom_call_target="tpu_custom_call" | custom-call | flops 524288 | bytes 2097152 | tf_op jit(solution)/shard_map/pallas_call | solution.py:54
  4.9 3.4 %copy.53 = f32[128,1,2176]{2,1,0:T(1,128)} copy(f32[128,1,2176]{2,0,1:T(8,128)} %bitcast.77) | data formatting | bytes 2228224 | tf_op jit(solution)/shard_map/all_to_all | solution.py:59
  8.3 11.5 %all-to-all-start = ((f32[128,1,2176]{2,1,0:T(1,128)}), f32[128,1,2176]{2,1,0:T(1,128)S(1)}, u32[]{:S(2)}, u32[]{:S(2)}) async-start(f32[128,1,2176]{2,1,0:T(1,128)} %copy.53), calls=%async_computation | async-start | bytes 2228224 | tf_op jit(solution)/shard_map/all_to_all | solution.py:59
  20.0 3.9 %fusion.44 = f32[512,512]{1,0:T(8,128)S(1)} fusion(), kind=kLoop, calls=%fused_computation.64 | loop fusion | flops 3932160 | bytes 1048576 | tf_op jit(solution)/shard_map/neg | solution.py:76
  23.9 5.0 %fusion.42 = (f32[512,512]{1,0:T(8,128)}, f32[512,512]{1,0:T(8,128)}) fusion(), kind=kLoop, calls=%fused_computation.62 | loop fusion | flops 3670016 | bytes 2097152 | tf_op jit(solution)/shard_map/sin | solution.py:19
  28.8 11.1 %all-to-all-done = f32[128,1,2176]{2,1,0:T(1,128)S(1)} async-done(((f32[128,1,2176]{2,1,0:T(1,128)}), f32[128,1,2176]{2,1,0:T(1,128)S(1)}, u32[]{:S(2)}, u32[]{:S(2)}) %all-to-all-start) | async-done | bytes 1114144 | tf_op jit(solution)/shard_map/all_to_all | solution.py:59
  40.2 0.4 reshape.124
  40.9 0.4 reshape.126
  41.3 0.4 multiply_reduce_fusion
  41.7 0.3 copy.55
  42.0 0.3 copy.54
  42.3 0.9 fusion.41
  43.3 1.3 %multiply_add_fusion = (f32[17,34,512]{2,0,1:T(8,128)S(1)}, f32[17,34,512]{2,0,1:T(8,128)S(1)}) fusion(f32[17,34,512]{2,0,1:T(8,128)S(1)} %fusion.41, f32[17,512]{1,0:T(8,128)S(1)} %get-tuple-element.27, f32[17,512]{1,0:T(8,128)S(1)} %get-tuple-element.28, f32[16,2,512]{2,0,1:T(8,128)S(1)} %reshape.129, f32[16,16,512]{2,0,1:T(8,128)S(1)} %bitcast.71, ...), kind=kOutput, calls=%fused_computation.27 | convolution fusion | flops 30746608 | bytes 4734976 | tf_op jit(solution)/shard_map/ks,scr->kcr/dot_general | solution.py:23
  44.6 0.3 pad_maximum_fusion.6
  44.9 0.9 copy-done.1
  45.8 0.3 copy-done.2
  46.1 5.7 %fusion.2 = f32[17,34,1024]{2,1,0:T(8,128)S(1)} fusion(f32[512,512]{1,0:T(8,128)S(1)} %copy-done.2, f32[512,512]{1,0:T(8,128)S(1)} %copy-done.1, f32[512,512]{1,0:T(8,128)S(1)} %fusion.44, f32[17,34,1024]{2,0,1:T(8,128)S(1)} %pad_maximum_fusion.6), kind=kOutput, calls=%fused_computation.6 | convolution fusion | flops 3639607296 | bytes 7880704 | tf_op jit(solution)/shard_map/kcn,nm->kcm/dot_general | solution.py:23
  51.8 0.2 multiply_add_fusion.1
  52.2 0.4 multiply_subtract_fusion.3
  52.6 0.4 fusion.29
  53.0 0.3 pad_maximum_fusion.7
  53.3 6.8 %fusion.6 = f32[17,34,1024]{2,0,1:T(8,128)S(1)} fusion(f32[512,512]{1,0:T(8,128)S(1)} %copy-done.2, f32[512,512]{1,0:T(8,128)S(1)} %fusion.44, f32[512,512]{1,0:T(8,128)S(1)} %copy-done.1, f32[17,34,1024]{2,1,0:T(8,128)S(1)} %pad_maximum_fusion.7), kind=kOutput, calls=%fused_computation.9 | convolution fusion | flops 3639607296 | bytes 7880704 | tf_op jit(solution)/shard_map/kcn,nm->kcm/dot_general | solution.py:23
  60.1 0.8 fusion.14
  60.9 0.8 fusion.26
  61.9 0.3 copy.60
  62.2 0.3 copy.61
  62.7 1.1 %all_to_all.15 = f32[128,1,3200]{2,1,0:T(1,128)S(1)} reshape(f32[128,3200]{1,0:T(8,128)S(1)} %pad_maximum_fusion.8) | data formatting | bytes 3276800 | tf_op jit(solution)/shard_map/all_to_all | solution.py:122
  63.9 29.4 %all_to_all.20 = f32[128,1,3200]{2,1,0:T(1,128)S(1)} all-to-all(f32[128,1,3200]{2,1,0:T(1,128)S(1)} %all_to_all.15), channel_id=1, replica_groups=mesh['seq'=16,'chan'=8] {'seq','chan'}, dimensions={0} | all-to-all | bytes 3276800 | tf_op jit(solution)/shard_map/all_to_all | solution.py:122
  93.2 1.3 %copy.78 = f32[128,1,3200]{2,0,1:T(8,128)} copy(f32[128,1,3200]{2,1,0:T(1,128)S(1)} %all_to_all.20) | data formatting | bytes 3276800
  94.5 3.1 %shard_map.102 = (bf16[512,256]{1,0:T(8,128)(2,1)}, bf16[512,256]{1,0:T(8,128)(2,1)}, bf16[512,256]{1,0:T(8,128)(2,1)}, f32[512,256]{1,0:T(8,128)}, f32[2,128]{1,0:T(2,128)}) custom-call(f32[128,3200]{1,0:T(8,128)} %bitcast.68, bf16[512,256]{1,0:T(8,128)(2,1)} %gi.3, bf16[512,256]{1,0:T(8,128)(2,1)} %vi.3, bf16[512,256]{1,0:T(8,128)(2,1)} %og.3, ...), custom_call_target="tpu_custom_call" | custom-call | flops 1572864 | bytes 4194304 | tf_op jit(solution)/shard_map/pallas_call | solution.py:142
  (25 shorter events, 1.3 us)
Async XLA Ops:
  0.6 1.0 %copy-start = (f32[512,256]{1,0:T(8,128)S(1)}, f32[512,256]{1,0:T(8,128)}, u32[]{:S(2)}) copy-start(f32[512,256]{1,0:T(8,128)} %param.11) | copy-start | bytes 1572868
  8.3 31.7 %all-to-all-start = ((f32[128,1,2176]{2,1,0:T(1,128)}), f32[128,1,2176]{2,1,0:T(1,128)S(1)}, u32[]{:S(2)}, u32[]{:S(2)}) async-start(f32[128,1,2176]{2,1,0:T(1,128)} %copy.53), calls=%async_computation | async-start | bytes 2228224 | tf_op jit(solution)/shard_map/all_to_all | solution.py:59
  44.5 1.2 %copy-start.1 = (f32[512,512]{1,0:T(8,128)S(1)}, f32[512,512]{1,0:T(8,128)}, u32[]{:S(2)}) copy-start(f32[512,512]{1,0:T(8,128)} %get-tuple-element.29) | copy-start | bytes 3145732
  44.6 1.5 %copy-start.2 = (f32[512,512]{1,0:T(8,128)S(1)}, f32[512,512]{1,0:T(8,128)}, u32[]{:S(2)}) copy-start(f32[512,512]{1,0:T(8,128)} %get-tuple-element.30) | copy-start | bytes 3145732

commit v3 on v2

--- a/solution.py
+++ b/solution.py
@@ -42,20 +42,26 @@
     taps_rows = lax.dynamic_slice_in_dim(filter_taps, chan_id * part, part, axis=0)
     taps_send = taps_rows.T.reshape(per_dev, dev_n, part).transpose(1, 0, 2).reshape(dev_n, per_dev * part)
 
+    lane = 128
+    send_w = (2 * span + per_dev * part) // lane
+    back_w = (3 * span + pad_w) // lane
+    rq = rows // lane
+
     def prep_kernel(gi, vi, og, ot, tr, send):
         for f2 in range(per_dev):
             lanes = pl.ds(f2 * dev_n, dev_n)
-            m = (gi[:, lanes].astype(F32) * vi[:, lanes].astype(F32)).astype(jnp.bfloat16).astype(F32)
-            g = (og[:, lanes].astype(F32) * ot[:, lanes].astype(F32)).astype(jnp.bfloat16).astype(F32)
-            send[:, pl.ds(f2 * rows, rows)] = m.T
-            send[:, pl.ds(span + f2 * rows, rows)] = g.T
-        send[:, pl.ds(2 * span, per_dev * part)] = tr[...]
+            m = (gi[:, lanes].astype(F32) * vi[:, lanes].astype(F32)).astype(jnp.bfloat16).astype(F32).T
+            g = (og[:, lanes].astype(F32) * ot[:, lanes].astype(F32)).astype(jnp.bfloat16).astype(F32).T
+            for q in range(rq):
+                send[pl.ds(f2 * rq + q, dev_n, stride=send_w), :] = m[:, q * lane : (q + 1) * lane]
+                send[pl.ds((per_dev + f2) * rq + q, dev_n, stride=send_w), :] = g[:, q * lane : (q + 1) * lane]
+        send[pl.ds(2 * per_dev * rq, dev_n, stride=send_w), :] = tr[...]
 
     send = pl.pallas_call(
         prep_kernel,
-        out_shape=jax.ShapeDtypeStruct((dev_n, 2 * span + per_dev * part), F32),
+        out_shape=jax.ShapeDtypeStruct((dev_n * send_w, lane), F32),
         cost_estimate=pl.CostEstimate(flops=4 * rows * local_ch, transcendentals=0, bytes_accessed=4 * 2 * rows * local_ch * 2),
-    )(gate_in, value_in, out_grad, out_gate, taps_send)
+    )(gate_in, value_in, out_grad, out_gate, taps_send).reshape(dev_n, send_w * lane)
     recv = lax.all_to_all(send, ("seq", "chan"), 0, 0, tiled=True).reshape(seq_n, chan_n, -1)
 
     def by_filter(block):
@@ -121,11 +127,15 @@
     out_send = jnp.concatenate([conv_blk, corr_blk, taps_blk, skip_blk], axis=2)
     back = lax.all_to_all(out_send.reshape(dev_n, -1), ("seq", "chan"), 0, 0, tiled=True)
     def tail_kernel(bk, gi, vi, og, ot, sg, o_gg, o_gog, o_gv, o_taps, o_skip):
+        def field(first):
+            parts = [bk[pl.ds(first + q, dev_n, stride=back_w), :] for q in range(rq)]
+            return jnp.concatenate(parts, axis=1).T
+
         for f2 in range(per_dev):
             lanes = pl.ds(f2 * dev_n, dev_n)
-            conv = bk[:, pl.ds(f2 * rows, rows)].T
-            corr = bk[:, pl.ds(span + f2 * rows, rows)].T
-            o_taps[:, lanes] = bk[:, pl.ds(2 * span + f2 * rows, rows)].T
+            conv = field(f2 * rq)
+            corr = field((per_dev + f2) * rq)
+            o_taps[:, lanes] = field((2 * per_dev + f2) * rq)
             gate = gi[:, lanes].astype(F32)
             val = vi[:, lanes].astype(F32)
             outg = og[:, lanes].astype(F32)
@@ -136,7 +146,7 @@
             mix = corr + s * g
             o_gg[:, lanes] = (mix * val).astype(jnp.bfloat16)
             o_gv[:, lanes] = (mix * gate).astype(jnp.bfloat16)
-        o_skip[...] = bk[:, pl.ds(3 * span, pad_w)].T[:per_dev, :]
+        o_skip[...] = bk[pl.ds(3 * per_dev * rq, dev_n, stride=back_w), :].T[:per_dev, :]
 
     grad_shape = jax.ShapeDtypeStruct((rows, local_ch), jnp.bfloat16)
     grad_gate, grad_out_gate, grad_value, taps_grad, skip_two = pl.pallas_call(
@@ -149,7 +159,7 @@
             jax.ShapeDtypeStruct((per_dev, dev_n), F32),
         ),
         cost_estimate=pl.CostEstimate(flops=12 * rows * local_ch, transcendentals=0, bytes_accessed=4 * 4 * rows * local_ch * 2),
-    )(back, gate_in, value_in, out_grad, out_gate, skip_gain.reshape(1, local_ch))
+    )(back.reshape(dev_n * back_w, lane), gate_in, value_in, out_grad, out_gate, skip_gain.reshape(1, local_ch))
     skip_grad = skip_two.reshape(local_ch)
     return (grad_gate, grad_out_gate, grad_value, skip_grad, taps_grad)
 

time: 98 us -> 93.3 us (0.952)
  local copies, waits for them, and re-layouts: 11.8 us -> 7.01 us
    all_to_all x1 -> x0, local copies, waits for them, and re-layouts: 3.38 us -> none  [body(): lax.all_to_all(send, ('seq', 'chan'), 0, 0, tiled=True)]
    unnamed x11 -> x8, local copies, waits for them, and re-layouts: 3.76 us -> 2.32 us
  transfers between devices with their start and end apart: 1 -> 1, of which waited for: 1 -> 1; matrix products, arithmetic and copies ran while one was open for 9% -> 10% of each run, Pallas kernels for 0% -> 0%
where the time goes in v3:
time: 93.3 us; the launch traced here: 93 us
  blocking collectives  29.5 us (32%)
  matrix products  16.3 us (17%)
  starting transfers between devices  11.5 us (12%)
  other arithmetic  11.2 us (12%)
  waiting for transfers between devices  11.1 us (12%)
  local copies, waits for them, and re-layouts  7.01 us (8%)
  Pallas kernels  5.5 us (6%)
    all_to_all x1, blocking collectives, body(): lax.all_to_all(out_send.reshape(dev_n, -1), ('seq', 'chan'), 0, 0, tiled=...  29.5 us
    dot_general x6, matrix products, mm(): return jnp.einsum(spec, a, b, precision=HIGH, preferred_element_type=F32)  16.3 us
    all_to_all x1, starting transfers between devices, body(): lax.all_to_all(send, ('seq', 'chan'), 0, 0, tiled=True)  11.5 us
    all_to_all x1, waiting for transfers between devices, body(): lax.all_to_all(send, ('seq', 'chan'), 0, 0, tiled=True)  11.1 us
    sin x2, other arithmetic, trig(): return (jnp.cos(angle) * scale, jnp.sin(angle) * scale)  5.18 us
    neg x1, other arithmetic, body(): -s2  3.85 us
    pallas_call x1, Pallas kernels, body(): pl.pallas_call(tail_kernel, out_shape=(grad_shape, grad_shape, grad_shape...  3.1 us
    pallas_call x1, Pallas kernels, body(): pl.pallas_call(prep_kernel, out_shape=jax.ShapeDtypeStruct((dev_n * send_...  2.39 us
  transfers between devices with their start and end apart: 1, of which 1 were waited for; matrix products, arithmetic and copies ran while one was open for 10% of the time, Pallas kernels for 0%

profile of v3, /device:TPU:1, one launch (start us, length us, event | category | flops | bytes accessed | tf_op | source)
XLA Modules:
  0.0 93.0 jit_solution(1850455761514701732)
XLA Ops:
  0.7 1.0 %copy-done = f32[512,256]{1,0:T(8,128)S(1)} copy-done((f32[512,256]{1,0:T(8,128)S(1)}, f32[512,256]{1,0:T(8,128)}, u32[]{:S(2)}) %copy-start) | copy-done | bytes 524312
  1.7 0.7 copy.39.tr
  2.5 2.4 %shard_map.101 = f32[2176,128]{1,0:T(8,128)} custom-call(bf16[512,256]{1,0:T(8,128)(2,1)} %gi.3, bf16[512,256]{1,0:T(8,128)(2,1)} %vi.3, bf16[512,256]{1,0:T(8,128)(2,1)} %og.3, bf16[512,256]{1,0:T(8,128)(2,1)} %ot.3, f32[128,128]{1,0:T(8,128)} %copy.39.tr), custom_call_target="tpu_custom_call" | custom-call | flops 524288 | bytes 2097152 | tf_op jit(solution)/shard_map/pallas_call | solution.py:60
  4.9 11.5 %all-to-all-start = ((f32[128,1,2176]{2,1,0:T(1,128)}), f32[128,1,2176]{2,1,0:T(1,128)S(1)}, u32[]{:S(2)}, u32[]{:S(2)}) async-start(f32[128,1,2176]{2,1,0:T(1,128)} %bitcast.73), calls=%async_computation | async-start | bytes 2228224 | tf_op jit(solution)/shard_map/all_to_all | solution.py:65
  16.4 0.2 fusion.51
  16.6 3.9 %fusion.44 = f32[512,512]{1,0:T(8,128)S(1)} fusion(), kind=kLoop, calls=%fused_computation.63 | loop fusion | flops 3932160 | bytes 1048576 | tf_op jit(solution)/shard_map/neg | solution.py:82
  20.4 5.0 %fusion.42 = (f32[512,512]{1,0:T(8,128)}, f32[512,512]{1,0:T(8,128)}) fusion(), kind=kLoop, calls=%fused_computation.61 | loop fusion | flops 3670016 | bytes 2097152 | tf_op jit(solution)/shard_map/sin | solution.py:19
  25.4 11.1 %all-to-all-done = f32[128,1,2176]{2,1,0:T(1,128)S(1)} async-done(((f32[128,1,2176]{2,1,0:T(1,128)}), f32[128,1,2176]{2,1,0:T(1,128)S(1)}, u32[]{:S(2)}, u32[]{:S(2)}) %all-to-all-start) | async-done | bytes 1114144 | tf_op jit(solution)/shard_map/all_to_all | solution.py:65
  36.7 0.4 reshape.130
  37.2 0.1 reshape.134
  37.4 0.4 reshape.132
  37.9 0.4 multiply_reduce_fusion
  38.3 0.3 copy.42
  38.6 0.3 copy.41
  38.9 0.9 %fusion.41 = f32[17,34,512]{2,0,1:T(8,128)S(1)} fusion(f32[16,2,512]{2,0,1:T(8,128)S(1)} %reshape.135, f32[16,16,512]{2,0,1:T(8,128)S(1)} %bitcast.68, f32[16,16,512]{2,0,1:T(8,128)S(1)} %bitcast.70), kind=kOutput, calls=%fused_computation.52 | convolution fusion | flops 28970720 | bytes 2297856 | tf_op jit(solution)/shard_map/ks,scr->kcr/dot_general | solution.py:23
  39.9 1.3 %multiply_add_fusion = (f32[17,34,512]{2,0,1:T(8,128)S(1)}, f32[17,34,512]{2,0,1:T(8,128)S(1)}) fusion(f32[17,34,512]{2,0,1:T(8,128)S(1)} %fusion.41, f32[17,512]{1,0:T(8,128)S(1)} %get-tuple-element.27, f32[17,512]{1,0:T(8,128)S(1)} %get-tuple-element.28, f32[16,2,512]{2,0,1:T(8,128)S(1)} %reshape.135, f32[16,16,512]{2,0,1:T(8,128)S(1)} %bitcast.69, ...), kind=kOutput, calls=%fused_computation.27 | convolution fusion | flops 30746608 | bytes 4734976 | tf_op jit(solution)/shard_map/ks,scr->kcr/dot_general | solution.py:23
  41.2 0.3 pad_maximum_fusion.6
  41.5 0.9 copy-done.1
  42.4 0.3 copy-done.2
  42.7 5.7 %fusion.2 = f32[17,34,1024]{2,1,0:T(8,128)S(1)} fusion(f32[512,512]{1,0:T(8,128)S(1)} %copy-done.2, f32[512,512]{1,0:T(8,128)S(1)} %copy-done.1, f32[512,512]{1,0:T(8,128)S(1)} %fusion.44, f32[17,34,1024]{2,0,1:T(8,128)S(1)} %pad_maximum_fusion.6), kind=kOutput, calls=%fused_computation.6 | convolution fusion | flops 3639607296 | bytes 7880704 | tf_op jit(solution)/shard_map/kcn,nm->kcm/dot_general | solution.py:23
  48.4 0.2 multiply_add_fusion.1
  48.8 0.4 multiply_subtract_fusion.3
  49.2 0.4 fusion.29
  49.6 0.3 pad_maximum_fusion.7
  49.9 6.8 %fusion.6 = f32[17,34,1024]{2,0,1:T(8,128)S(1)} fusion(f32[512,512]{1,0:T(8,128)S(1)} %copy-done.2, f32[512,512]{1,0:T(8,128)S(1)} %fusion.44, f32[512,512]{1,0:T(8,128)S(1)} %copy-done.1, f32[17,34,1024]{2,1,0:T(8,128)S(1)} %pad_maximum_fusion.7), kind=kOutput, calls=%fused_computation.9 | convolution fusion | flops 3639607296 | bytes 7880704 | tf_op jit(solution)/shard_map/kcn,nm->kcm/dot_general | solution.py:23
  56.7 0.8 fusion.14
  57.5 0.8 fusion.26
  58.4 0.3 copy.47
  58.7 0.3 copy.48
  59.2 1.1 %all_to_all.14 = f32[128,1,3200]{2,1,0:T(1,128)S(1)} reshape(f32[128,3200]{1,0:T(8,128)S(1)} %pad_maximum_fusion.8) | data formatting | bytes 3276800 | tf_op jit(solution)/shard_map/all_to_all | solution.py:128
  60.4 29.5 %all_to_all.18 = f32[128,1,3200]{2,1,0:T(1,128)} all-to-all(f32[128,1,3200]{2,1,0:T(1,128)S(1)} %all_to_all.14), channel_id=1, replica_groups=mesh['seq'=16,'chan'=8] {'seq','chan'}, dimensions={0} | all-to-all | bytes 3276800 | tf_op jit(solution)/shard_map/all_to_all | solution.py:128
  89.9 3.1 %shard_map.102 = (bf16[512,256]{1,0:T(8,128)(2,1)}, bf16[512,256]{1,0:T(8,128)(2,1)}, bf16[512,256]{1,0:T(8,128)(2,1)}, f32[512,256]{1,0:T(8,128)}, f32[2,128]{1,0:T(2,128)}) custom-call(f32[3200,128]{1,0:T(8,128)} %bitcast.66, bf16[512,256]{1,0:T(8,128)(2,1)} %gi.3, bf16[512,256]{1,0:T(8,128)(2,1)} %vi.3, bf16[512,256]{1,0:T(8,128)(2,1)} %og.3, ...), custom_call_target="tpu_custom_call" | custom-call | flops 1572864 | bytes 4194304 | tf_op jit(solution)/shard_map/pallas_call | solution.py:152
  (21 shorter events, 0.8 us)
Async XLA Ops:
  0.6 1.0 %copy-start = (f32[512,256]{1,0:T(8,128)S(1)}, f32[512,256]{1,0:T(8,128)}, u32[]{:S(2)}) copy-start(f32[512,256]{1,0:T(8,128)} %param.11) | copy-start | bytes 1572868
  4.9 31.7 %all-to-all-start = ((f32[128,1,2176]{2,1,0:T(1,128)}), f32[128,1,2176]{2,1,0:T(1,128)S(1)}, u32[]{:S(2)}, u32[]{:S(2)}) async-start(f32[128,1,2176]{2,1,0:T(1,128)} %bitcast.73), calls=%async_computation | async-start | bytes 2228224 | tf_op jit(solution)/shard_map/all_to_all | solution.py:65
  41.1 1.2 %copy-start.1 = (f32[512,512]{1,0:T(8,128)S(1)}, f32[512,512]{1,0:T(8,128)}, u32[]{:S(2)}) copy-start(f32[512,512]{1,0:T(8,128)} %get-tuple-element.29) | copy-start | bytes 3145732
  41.1 1.5 %copy-start.2 = (f32[512,512]{1,0:T(8,128)S(1)}, f32[512,512]{1,0:T(8,128)}, u32[]{:S(2)}) copy-start(f32[512,512]{1,0:T(8,128)} %get-tuple-element.30) | copy-start | bytes 3145732

commit v4 on v3

--- a/solution.py
+++ b/solution.py
@@ -64,20 +64,28 @@
     )(gate_in, value_in, out_grad, out_gate, taps_send).reshape(dev_n, send_w * lane)
     recv = lax.all_to_all(send, ("seq", "chan"), 0, 0, tiled=True).reshape(seq_n, chan_n, -1)
 
-    def by_filter(block):
-        return block.reshape(seq_n, chan_n, per_dev, rows).transpose(0, 2, 1, 3).reshape(seq_n, cc, rows)
+    qn = rows // lane
+    blocks = seq_n * qn
+    k1 = blocks + 1
+    length = 2 * blocks * lane
+    recv = recv.reshape(seq_n, chan_n, send_w, lane)
 
-    m_pos = by_filter(recv[:, :, :span])
-    g_pos = by_filter(recv[:, :, span : 2 * span])
-    h_pos = recv[:, :, 2 * span :].reshape(seq_n, chan_n, per_dev, part)
-    h_pos = h_pos.transpose(0, 2, 1, 3).reshape(seq_n, per_dev, rows)
+    def by_block(field):
+        part_rows = recv[:, :, field * per_dev * qn : (field + 1) * per_dev * qn]
+        part_rows = part_rows.reshape(seq_n, chan_n, per_dev, qn, lane).transpose(0, 3, 2, 1, 4)
+        return part_rows.reshape(blocks, cc, lane)
+
+    m_pos = by_block(0)
+    g_pos = by_block(1)
+    h_pos = recv[:, :, 2 * per_dev * qn].reshape(seq_n, qn, lane // part, per_dev, part)
+    h_pos = h_pos.transpose(0, 1, 3, 2, 4).reshape(blocks, per_dev, lane)
     skip_mine = jnp.sum(m_pos * g_pos, axis=(0, 2)).reshape(per_dev, chan_n).T
 
-    c1, s1 = trig(k1, seq_n, 2 * seq_n)
-    tw_c, tw_s = trig(k1, rows, length)
+    c1, s1 = trig(k1, blocks, 2 * blocks)
+    tw_c, tw_s = trig(k1, lane, length)
     tw_c = tw_c[:, None, :]
     tw_s = tw_s[:, None, :]
-    c2, s2 = trig(rows, rows, rows)
+    c2, s2 = trig(lane, lane, lane)
     w_fwd = jnp.concatenate(
         [jnp.concatenate([c2, -s2], axis=1), jnp.concatenate([s2, c2], axis=1)], axis=0
     )
@@ -85,9 +93,9 @@
         [jnp.concatenate([c2, s2], axis=1), jnp.concatenate([-s2, c2], axis=1)], axis=0
     )
     weight = jnp.where(
-        (lax.iota(jnp.int32, k1) == 0) | (lax.iota(jnp.int32, k1) == seq_n), 1.0, 2.0
+        (lax.iota(jnp.int32, k1) == 0) | (lax.iota(jnp.int32, k1) == blocks), 1.0, 2.0
     ) / length
-    ci, si = trig(seq_n, k1, 2 * seq_n)
+    ci, si = trig(blocks, k1, 2 * blocks)
     ci = ci * weight[None, :]
     si = si * weight[None, :]
 
@@ -97,35 +105,37 @@
     turned = jnp.concatenate([are * tw_c + aim * tw_s, aim * tw_c - are * tw_s], axis=2)
     spec = mm("kcn,nm->kcm", turned, w_fwd)
 
-    mre, mim = spec[:, :cc, :rows], spec[:, :cc, rows:]
-    gre, gim = spec[:, cc : 2 * cc, :rows], spec[:, cc : 2 * cc, rows:]
+    mre, mim = spec[:, :cc, :lane], spec[:, :cc, lane:]
+    gre, gim = spec[:, cc : 2 * cc, :lane], spec[:, cc : 2 * cc, lane:]
     h = spec[:, 2 * cc :]
-    h = jnp.broadcast_to(h[:, :, None, :], (k1, per_dev, chan_n, 2 * rows)).reshape(k1, cc, 2 * rows)
-    hre, him = h[:, :, :rows], h[:, :, rows:]
+    h = jnp.broadcast_to(h[:, :, None, :], (k1, per_dev, chan_n, 2 * lane)).reshape(k1, cc, 2 * lane)
+    hre, him = h[:, :, :lane], h[:, :, lane:]
 
     conv_s = jnp.concatenate([hre * mre - him * mim, hre * mim + him * mre], axis=2)
     corr_s = jnp.concatenate([gre * hre + gim * him, gim * hre - gre * him], axis=2)
     taps_s = jnp.concatenate([gre * mre + gim * mim, gim * mre - gre * mim], axis=2)
-    taps_s = jnp.sum(taps_s.reshape(k1, per_dev, chan_n, 2 * rows), axis=2)
+    taps_s = jnp.sum(taps_s.reshape(k1, per_dev, chan_n, 2 * lane), axis=2)
 
     prod = jnp.concatenate([conv_s, corr_s, taps_s], axis=1)
     z = mm("kcn,nm->kcm", prod, w_inv)
-    zre, zim = z[:, :, :rows], z[:, :, rows:]
+    zre, zim = z[:, :, :lane], z[:, :, lane:]
     ure = zre * tw_c - zim * tw_s
     uim = zre * tw_s + zim * tw_c
     y = mm("ik,kcr->icr", ci, ure) - mm("ik,kcr->icr", si, uim)
 
-    def by_copy(block):
-        return block.reshape(seq_n, per_dev, chan_n, rows).transpose(0, 2, 1, 3).reshape(seq_n, chan_n, span)
+    def by_chunk(block, copies):
+        block = block.reshape(seq_n, qn, per_dev, copies, lane).transpose(0, 3, 2, 1, 4)
+        return block.reshape(seq_n, copies, span)
 
-    conv_blk = by_copy(y[:, :cc])
-    corr_blk = by_copy(y[:, cc : 2 * cc])
-    taps_blk = jnp.broadcast_to(y[:, 2 * cc :].reshape(seq_n, 1, span), (seq_n, chan_n, span))
+    conv_blk = by_chunk(y[:, :cc], chan_n)
+    corr_blk = by_chunk(y[:, cc : 2 * cc], chan_n)
+    taps_blk = jnp.broadcast_to(by_chunk(y[:, 2 * cc :], 1), (seq_n, chan_n, span))
     skip_blk = jnp.broadcast_to(
         jnp.pad(skip_mine, ((0, 0), (0, pad_w - per_dev)))[None], (seq_n, chan_n, pad_w)
     )
     out_send = jnp.concatenate([conv_blk, corr_blk, taps_blk, skip_blk], axis=2)
     back = lax.all_to_all(out_send.reshape(dev_n, -1), ("seq", "chan"), 0, 0, tiled=True)
+
     def tail_kernel(bk, gi, vi, og, ot, sg, o_gg, o_gog, o_gv, o_taps, o_skip):
         def field(first):
             parts = [bk[pl.ds(first + q, dev_n, stride=back_w), :] for q in range(rq)]

time: 93.3 us -> 79.1 us (0.85)
  matrix products: 16.3 us -> 5.84 us
  other arithmetic: 11.2 us -> 1.44 us
  waiting for transfers between devices: 11.1 us -> 19.5 us
  local copies, waits for them, and re-layouts: 7.01 us -> 4.73 us
    dot_general x6, matrix products: 16.3 us -> 5.84 us  [mm(): return jnp.einsum(spec, a, b, precision=HIGH, preferred_element_type=F32)]
    all_to_all x1, waiting for transfers between devices: 11.1 us -> 19.5 us  [body(): lax.all_to_all(send, ('seq', 'chan'), 0, 0, tiled=True)]
    sin x2, other arithmetic: 5.18 us -> 0.44 us  [trig(): return (jnp.cos(angle) * scale, jnp.sin(angle) * scale)]
    neg x1, other arithmetic: 3.85 us -> 0.26 us  [body(): -s2]
    unnamed x8 -> x3, local copies, waits for them, and re-layouts: 2.32 us -> 1.12 us
    reshape x5 -> x2, local copies, waits for them, and re-layouts: 1.22 us -> 0.14 us  [the longest x1 0.13 us: body(): h_pos = h_pos.transpose(0, 1, 3, 2, 4).reshape(blocks, per_dev, lane)]
  transfers between devices with their start and end apart: 1 -> 1, of which waited for: 1 -> 1; matrix products, arithmetic and copies ran while one was open for 10% -> 1% of each run, Pallas kernels for 0% -> 0%
where the time goes in v4:
time: 79.1 us; the launch traced here: 78.9 us
  blocking collectives  29.5 us (37%)
  waiting for transfers between devices  19.5 us (25%)
  starting transfers between devices  11.5 us (15%)
  matrix products  5.84 us (7%)
  Pallas kernels  5.5 us (7%)
  local copies, waits for them, and re-layouts  4.73 us (6%)
  other arithmetic  1.44 us (2%)
  between operations  0.89 us (1%)
    all_to_all x1, blocking collectives, body(): lax.all_to_all(out_send.reshape(dev_n, -1), ('seq', 'chan'), 0, 0, tiled=...  29.5 us
    all_to_all x1, waiting for transfers between devices, body(): lax.all_to_all(send, ('seq', 'chan'), 0, 0, tiled=True)  19.5 us
    all_to_all x1, starting transfers between devices, body(): lax.all_to_all(send, ('seq', 'chan'), 0, 0, tiled=True)  11.5 us
    dot_general x6, matrix products, mm(): return jnp.einsum(spec, a, b, precision=HIGH, preferred_element_type=F32)  5.84 us
    pallas_call x1, Pallas kernels, body(): pl.pallas_call(tail_kernel, out_shape=(grad_shape, grad_shape, grad_shape...  3.1 us
    pallas_call x1, Pallas kernels, body(): pl.pallas_call(prep_kernel, out_shape=jax.ShapeDtypeStruct((dev_n * send_...  2.39 us
  transfers between devices with their start and end apart: 1, of which 1 were waited for; matrix products, arithmetic and copies ran while one was open for 1% of the time, Pallas kernels for 0%

profile of v4, /device:TPU:1, one launch (start us, length us, event | category | flops | bytes accessed | tf_op | source)
XLA Modules:
  0.0 78.9 jit_solution(9437802979294286156)
XLA Ops:
  0.7 1.0 %copy-done = f32[512,256]{1,0:T(8,128)S(1)} copy-done((f32[512,256]{1,0:T(8,128)S(1)}, f32[512,256]{1,0:T(8,128)}, u32[]{:S(2)}) %copy-start) | copy-done | bytes 524312
  1.7 0.7 copy.40.tr
  2.5 2.4 %shard_map.101 = f32[2176,128]{1,0:T(8,128)} custom-call(bf16[512,256]{1,0:T(8,128)(2,1)} %gi.3, bf16[512,256]{1,0:T(8,128)(2,1)} %vi.3, bf16[512,256]{1,0:T(8,128)(2,1)} %og.3, bf16[512,256]{1,0:T(8,128)(2,1)} %ot.3, f32[128,128]{1,0:T(8,128)} %copy.40.tr), custom_call_target="tpu_custom_call" | custom-call | flops 524288 | bytes 2097152 | tf_op jit(solution)/shard_map/pallas_call | solution.py:60
  4.9 11.5 %all-to-all-start = ((f32[128,1,2176]{2,1,0:T(1,128)}), f32[128,1,2176]{2,1,0:T(1,128)S(1)}, u32[]{:S(2)}, u32[]{:S(2)}) async-start(f32[128,1,2176]{2,1,0:T(1,128)} %bitcast.80), calls=%async_computation | async-start | bytes 2228224 | tf_op jit(solution)/shard_map/all_to_all | solution.py:65
  16.4 0.3 fusion.78
  16.6 0.2 fusion.79
  16.8 0.3 fusion.65
  17.1 19.5 %all-to-all-done = f32[128,1,2176]{2,1,0:T(1,128)S(1)} async-done(((f32[128,1,2176]{2,1,0:T(1,128)}), f32[128,1,2176]{2,1,0:T(1,128)S(1)}, u32[]{:S(2)}, u32[]{:S(2)}) %all-to-all-start) | async-done | bytes 1114144 | tf_op jit(solution)/shard_map/all_to_all | solution.py:65
  36.5 0.1 copy.53
  36.6 0.1 fusion.109
  36.7 0.1 copy.44
  36.9 0.2 multiply_reduce_fusion
  37.1 0.1 copy.43
  37.2 0.1 reshape_squeeze.3
  37.4 0.1 reshape.130
  37.6 0.8 %fusion.26 = f32[65,34,128]{2,0,1:T(8,128)S(1)} fusion(f32[64,2,128]{2,0,1:T(8,128)S(1)} %reshape.130, f32[64,16,128]{2,0,1:T(8,128)S(1)} %bitcast.71, f32[64,16,128]{2,0,1:T(8,128)S(1)} %bitcast.73), kind=kOutput, calls=%fused_computation.34 | convolution fusion | flops 109241216 | bytes 2245632 | tf_op jit(solution)/shard_map/ks,scr->kcr/dot_general | solution.py:23
  38.4 1.1 %multiply_add_fusion = (f32[65,34,128]{2,0,1:T(8,128)S(1)}, f32[65,34,128]{2,0,1:T(8,128)S(1)}) fusion(f32[65,34,128]{2,0,1:T(8,128)S(1)} %fusion.26, f32[65,128]{1,0:T(8,128)S(1)} %get-tuple-element.27, f32[65,128]{1,0:T(8,128)S(1)} %get-tuple-element.28, f32[64,2,128]{2,0,1:T(8,128)S(1)} %reshape.130, f32[64,16,128]{2,0,1:T(8,128)S(1)} %bitcast.72, ...), kind=kOutput, calls=%fused_computation.24 | convolution fusion | flops 110942656 | bytes 4575232 | tf_op jit(solution)/shard_map/ks,scr->kcr/dot_general | solution.py:23
  39.5 1.2 %fusion = f32[65,34,256]{2,0,1:T(8,128)S(1)} fusion(f32[65,34,128]{2,0,1:T(8,128)S(1)} %get-tuple-element.20, f32[65,34,128]{2,0,1:T(8,128)S(1)} %get-tuple-element.19, f32[128,128]{1,0:T(8,128)S(1)} %get-tuple-element.30, f32[128,128]{1,0:T(8,128)S(1)} %get-tuple-element.29, f32[128,128]{1,0:T(8,128)S(1)} %fusion.78), kind=kOutput, calls=%fused_computation | convolution fusion | flops 869769728 | bytes 4722688 | tf_op jit(solution)/shard_map/kcn,nm->kcm/dot_general | solution.py:23
  40.7 0.1 multiply_add_fusion.1
  40.8 0.1 broadcast_in_dim.18
  40.9 0.2 multiply_subtract_fusion.3
  41.2 1.2 %fusion.4 = f32[65,34,256]{2,0,1:T(8,128)S(1)} fusion(f32[65,2,256]{2,0,1:T(8,128)S(1)} %bitcast_reduce_fusion, f32[65,16,128]{2,0,1:T(8,128)S(1)} %get-tuple-element.17, f32[65,16,128]{2,0,1:T(8,128)S(1)} %get-tuple-element.16, f32[65,16,128]{2,0,1:T(8,128)S(1)} %get-tuple-element.18, f32[65,16,128]{2,0,1:T(8,128)S(1)} %get-tuple-element.15, ...), kind=kOutput, calls=%fused_computation.4 | convolution fusion | flops 871467008 | bytes 4722688 | tf_op jit(solution)/shard_map/kcn,nm->kcm/dot_general | solution.py:23
  42.4 0.8 fusion.17
  43.2 0.8 %convolution_subtract_fusion = f32[64,34,128]{2,0,1:T(8,128)S(1)} fusion(f32[64,34,128]{2,0,1:T(8,128)S(1)} %fusion.17, f32[65,34,256]{2,0,1:T(8,128)S(1)} %fusion.4, f32[65,128]{1,0:T(8,128)S(1)} %get-tuple-element.27, f32[65,128]{1,0:T(8,128)S(1)} %get-tuple-element.28, f32[65]{0:T(128)S(1)} %fusion.87), kind=kOutput, calls=%fused_computation.15 | convolution fusion | flops 109815488 | bytes 4558084 | tf_op jit(solution)/shard_map/ik,kcr->icr/dot_general | solution.py:23
  44.0 0.1 fusion.108
  44.1 0.1 copy.50
  44.2 0.3 copy.46
  44.5 0.3 copy.47
  45.0 0.1 pad_maximum_fusion
  45.1 1.1 %all_to_all.14 = f32[128,1,3200]{2,1,0:T(1,128)S(1)} reshape(f32[128,3200]{1,0:T(8,128)S(1)} %pad_maximum_fusion) | data formatting | bytes 3276800 | tf_op jit(solution)/shard_map/all_to_all | solution.py:137
  46.2 29.5 %all_to_all.18 = f32[128,1,3200]{2,1,0:T(1,128)} all-to-all(f32[128,1,3200]{2,1,0:T(1,128)S(1)} %all_to_all.14), channel_id=1, replica_groups=mesh['seq'=16,'chan'=8] {'seq','chan'}, dimensions={0} | all-to-all | bytes 3276800 | tf_op jit(solution)/shard_map/all_to_all | solution.py:137
  75.7 3.1 %shard_map.102 = (bf16[512,256]{1,0:T(8,128)(2,1)}, bf16[512,256]{1,0:T(8,128)(2,1)}, bf16[512,256]{1,0:T(8,128)(2,1)}, f32[512,256]{1,0:T(8,128)}, f32[2,128]{1,0:T(2,128)}) custom-call(f32[3200,128]{1,0:T(8,128)} %bitcast.70, bf16[512,256]{1,0:T(8,128)(2,1)} %gi.3, bf16[512,256]{1,0:T(8,128)(2,1)} %vi.3, bf16[512,256]{1,0:T(8,128)(2,1)} %og.3, ...), custom_call_target="tpu_custom_call" | custom-call | flops 1572864 | bytes 4194304 | tf_op jit(solution)/shard_map/pallas_call | solution.py:162
  (15 shorter events, 0.3 us)
Async XLA Ops:
  0.6 1.0 %copy-start = (f32[512,256]{1,0:T(8,128)S(1)}, f32[512,256]{1,0:T(8,128)}, u32[]{:S(2)}) copy-start(f32[512,256]{1,0:T(8,128)} %param.11) | copy-start | bytes 1572868
  4.9 31.7 %all-to-all-start = ((f32[128,1,2176]{2,1,0:T(1,128)}), f32[128,1,2176]{2,1,0:T(1,128)S(1)}, u32[]{:S(2)}, u32[]{:S(2)}) async-start(f32[128,1,2176]{2,1,0:T(1,128)} %bitcast.80), calls=%async_computation | async-start | bytes 2228224 | tf_op jit(solution)/shard_map/all_to_all | solution.py:65

commit v5 on v4

--- a/solution.py
+++ b/solution.py
@@ -38,16 +38,13 @@
     cc = chan_n * per_dev
     pad_w = 128
 
-    chan_id = lax.axis_index("chan")
-    taps_rows = lax.dynamic_slice_in_dim(filter_taps, chan_id * part, part, axis=0)
-    taps_send = taps_rows.T.reshape(per_dev, dev_n, part).transpose(1, 0, 2).reshape(dev_n, per_dev * part)
 
     lane = 128
     send_w = (2 * span + per_dev * part) // lane
     back_w = (3 * span + pad_w) // lane
     rq = rows // lane
 
-    def prep_kernel(gi, vi, og, ot, tr, send):
+    def prep_kernel(gi, vi, og, ot, ft, send):
         for f2 in range(per_dev):
             lanes = pl.ds(f2 * dev_n, dev_n)
             m = (gi[:, lanes].astype(F32) * vi[:, lanes].astype(F32)).astype(jnp.bfloat16).astype(F32).T
@@ -55,13 +52,17 @@
             for q in range(rq):
                 send[pl.ds(f2 * rq + q, dev_n, stride=send_w), :] = m[:, q * lane : (q + 1) * lane]
                 send[pl.ds((per_dev + f2) * rq + q, dev_n, stride=send_w), :] = g[:, q * lane : (q + 1) * lane]
-        send[pl.ds(2 * per_dev * rq, dev_n, stride=send_w), :] = tr[...]
+        first = pl.multiple_of(lax.axis_index("chan") * part, part)
+        window = jnp.concatenate(
+            [ft[pl.ds(first, part), pl.ds(f2 * dev_n, dev_n)] for f2 in range(per_dev)], axis=0
+        )
+        send[pl.ds(2 * per_dev * rq, dev_n, stride=send_w), :] = window.T
 
     send = pl.pallas_call(
         prep_kernel,
         out_shape=jax.ShapeDtypeStruct((dev_n * send_w, lane), F32),
         cost_estimate=pl.CostEstimate(flops=4 * rows * local_ch, transcendentals=0, bytes_accessed=4 * 2 * rows * local_ch * 2),
-    )(gate_in, value_in, out_grad, out_gate, taps_send).reshape(dev_n, send_w * lane)
+    )(gate_in, value_in, out_grad, out_gate, filter_taps).reshape(dev_n, send_w * lane)
     recv = lax.all_to_all(send, ("seq", "chan"), 0, 0, tiled=True).reshape(seq_n, chan_n, -1)
 
     qn = rows // lane

time: 79.1 us -> 77.5 us (0.980)
  local copies, waits for them, and re-layouts: 4.73 us -> 2.92 us
    unnamed x3 -> x1, local copies, waits for them, and re-layouts: 1.12 us -> 0.08 us
where the time goes in v5:
time: 77.5 us; the launch traced here: 77.2 us
  blocking collectives  29.5 us (38%)
  waiting for transfers between devices  19.5 us (25%)
  starting transfers between devices  11.5 us (15%)
  matrix products  5.84 us (8%)
  Pallas kernels  5.7 us (7%)
  local copies, waits for them, and re-layouts  2.92 us (4%)
  other arithmetic  1.44 us (2%)
  between operations  0.86 us (1%)
    all_to_all x1, blocking collectives, body(): lax.all_to_all(out_send.reshape(dev_n, -1), ('seq', 'chan'), 0, 0, tiled=...  29.5 us
    all_to_all x1, waiting for transfers between devices, body(): lax.all_to_all(send, ('seq', 'chan'), 0, 0, tiled=True)  19.5 us
    all_to_all x1, starting transfers between devices, body(): lax.all_to_all(send, ('seq', 'chan'), 0, 0, tiled=True)  11.5 us
    dot_general x6, matrix products, mm(): return jnp.einsum(spec, a, b, precision=HIGH, preferred_element_type=F32)  5.84 us
    pallas_call x1, Pallas kernels, body(): pl.pallas_call(tail_kernel, out_shape=(grad_shape, grad_shape, grad_shape...  3.1 us
    pallas_call x1, Pallas kernels, body(): pl.pallas_call(prep_kernel, out_shape=jax.ShapeDtypeStruct((dev_n * send_...  2.6 us
  transfers between devices with their start and end apart: 1, of which 1 were waited for; matrix products, arithmetic and copies ran while one was open for 1% of the time, Pallas kernels for 0%

profile of v5, /device:TPU:1, one launch (start us, length us, event | category | flops | bytes accessed | tf_op | source)
XLA Modules:
  0.0 77.2 jit_solution(11979548264277460148)
XLA Ops:
  0.6 2.6 %shard_map.101 = f32[2176,128]{1,0:T(8,128)} custom-call(bf16[512,256]{1,0:T(8,128)(2,1)} %gi.3, bf16[512,256]{1,0:T(8,128)(2,1)} %vi.3, bf16[512,256]{1,0:T(8,128)(2,1)} %og.3, bf16[512,256]{1,0:T(8,128)(2,1)} %ot.3, f32[512,256]{1,0:T(8,128)} %ft.1), custom_call_target="tpu_custom_call" | custom-call | flops 524288 | bytes 2097152 | tf_op jit(solution)/shard_map/pallas_call | solution.py:61
  3.2 11.5 %all-to-all-start = ((f32[128,1,2176]{2,1,0:T(1,128)}), f32[128,1,2176]{2,1,0:T(1,128)S(1)}, u32[]{:S(2)}, u32[]{:S(2)}) async-start(f32[128,1,2176]{2,1,0:T(1,128)} %bitcast.74), calls=%async_computation | async-start | bytes 2228224 | tf_op jit(solution)/shard_map/all_to_all | solution.py:66
  14.7 0.3 fusion.78
  15.0 0.2 fusion.79
  15.2 0.3 fusion.65
  15.4 19.5 %all-to-all-done = f32[128,1,2176]{2,1,0:T(1,128)S(1)} async-done(((f32[128,1,2176]{2,1,0:T(1,128)}), f32[128,1,2176]{2,1,0:T(1,128)S(1)}, u32[]{:S(2)}, u32[]{:S(2)}) %all-to-all-start) | async-done | bytes 1114144 | tf_op jit(solution)/shard_map/all_to_all | solution.py:66
  34.9 0.1 copy.39
  35.0 0.1 fusion.109
  35.1 0.1 copy.30
  35.3 0.2 multiply_reduce_fusion
  35.4 0.1 copy.29
  35.6 0.1 reshape_squeeze.3
  35.7 0.1 copy.31
  35.8 0.1 reshape.122
  35.9 0.8 %fusion.26 = f32[65,34,128]{2,0,1:T(8,128)S(1)} fusion(f32[64,2,128]{2,0,1:T(8,128)S(1)} %reshape.122, f32[64,16,128]{2,0,1:T(8,128)S(1)} %bitcast.65, f32[64,16,128]{2,0,1:T(8,128)S(1)} %bitcast.67), kind=kOutput, calls=%fused_computation.34 | convolution fusion | flops 109241216 | bytes 2245632 | tf_op jit(solution)/shard_map/ks,scr->kcr/dot_general | solution.py:23
  36.8 1.1 %multiply_add_fusion = (f32[65,34,128]{2,0,1:T(8,128)S(1)}, f32[65,34,128]{2,0,1:T(8,128)S(1)}) fusion(f32[65,34,128]{2,0,1:T(8,128)S(1)} %fusion.26, f32[65,128]{1,0:T(8,128)S(1)} %get-tuple-element.27, f32[65,128]{1,0:T(8,128)S(1)} %get-tuple-element.28, f32[64,2,128]{2,0,1:T(8,128)S(1)} %reshape.122, f32[64,16,128]{2,0,1:T(8,128)S(1)} %bitcast.66, ...), kind=kOutput, calls=%fused_computation.24 | convolution fusion | flops 110942656 | bytes 4575232 | tf_op jit(solution)/shard_map/ks,scr->kcr/dot_general | solution.py:23
  37.9 1.2 %fusion = f32[65,34,256]{2,0,1:T(8,128)S(1)} fusion(f32[65,34,128]{2,0,1:T(8,128)S(1)} %get-tuple-element.20, f32[65,34,128]{2,0,1:T(8,128)S(1)} %get-tuple-element.19, f32[128,128]{1,0:T(8,128)S(1)} %get-tuple-element.30, f32[128,128]{1,0:T(8,128)S(1)} %get-tuple-element.29, f32[128,128]{1,0:T(8,128)S(1)} %fusion.78), kind=kOutput, calls=%fused_computation | convolution fusion | flops 869769728 | bytes 4722688 | tf_op jit(solution)/shard_map/kcn,nm->kcm/dot_general | solution.py:23
  39.1 0.1 multiply_add_fusion.1
  39.2 0.1 broadcast_in_dim.18
  39.3 0.2 multiply_subtract_fusion.3
  39.5 0.1 bitcast_reduce_fusion
  39.6 1.2 %fusion.4 = f32[65,34,256]{2,0,1:T(8,128)S(1)} fusion(f32[65,2,256]{2,0,1:T(8,128)S(1)} %bitcast_reduce_fusion, f32[65,16,128]{2,0,1:T(8,128)S(1)} %get-tuple-element.17, f32[65,16,128]{2,0,1:T(8,128)S(1)} %get-tuple-element.16, f32[65,16,128]{2,0,1:T(8,128)S(1)} %get-tuple-element.18, f32[65,16,128]{2,0,1:T(8,128)S(1)} %get-tuple-element.15, ...), kind=kOutput, calls=%fused_computation.4 | convolution fusion | flops 871467008 | bytes 4722688 | tf_op jit(solution)/shard_map/kcn,nm->kcm/dot_general | solution.py:23
  40.8 0.8 %fusion.17 = f32[64,34,128]{2,0,1:T(8,128)S(1)} fusion(f32[65,34,256]{2,0,1:T(8,128)S(1)} %fusion.4, f32[65,128]{1,0:T(8,128)S(1)} %get-tuple-element.27, f32[65,128]{1,0:T(8,128)S(1)} %get-tuple-element.28, f32[65]{0:T(128)S(1)} %fusion.87), kind=kOutput, calls=%fused_computation.19 | convolution fusion | flops 109536960 | bytes 3443972 | tf_op jit(solution)/shard_map/ik,kcr->icr/dot_general | solution.py:23
  41.6 0.8 %convolution_subtract_fusion = f32[64,34,128]{2,0,1:T(8,128)S(1)} fusion(f32[64,34,128]{2,0,1:T(8,128)S(1)} %fusion.17, f32[65,34,256]{2,0,1:T(8,128)S(1)} %fusion.4, f32[65,128]{1,0:T(8,128)S(1)} %get-tuple-element.27, f32[65,128]{1,0:T(8,128)S(1)} %get-tuple-element.28, f32[65]{0:T(128)S(1)} %fusion.87), kind=kOutput, calls=%fused_computation.15 | convolution fusion | flops 109815488 | bytes 4558084 | tf_op jit(solution)/shard_map/ik,kcr->icr/dot_general | solution.py:23
  42.4 0.1 fusion.108
  42.5 0.1 copy.36
  42.6 0.3 copy.32
  42.9 0.3 copy.33
  43.3 0.1 pad_maximum_fusion
  43.5 1.1 %all_to_all.14 = f32[128,1,3200]{2,1,0:T(1,128)S(1)} reshape(f32[128,3200]{1,0:T(8,128)S(1)} %pad_maximum_fusion) | data formatting | bytes 3276800 | tf_op jit(solution)/shard_map/all_to_all | solution.py:138
  44.6 29.5 %all_to_all.18 = f32[128,1,3200]{2,1,0:T(1,128)} all-to-all(f32[128,1,3200]{2,1,0:T(1,128)S(1)} %all_to_all.14), channel_id=1, replica_groups=mesh['seq'=16,'chan'=8] {'seq','chan'}, dimensions={0} | all-to-all | bytes 3276800 | tf_op jit(solution)/shard_map/all_to_all | solution.py:138
  74.1 3.1 %shard_map.102 = (bf16[512,256]{1,0:T(8,128)(2,1)}, bf16[512,256]{1,0:T(8,128)(2,1)}, bf16[512,256]{1,0:T(8,128)(2,1)}, f32[512,256]{1,0:T(8,128)}, f32[2,128]{1,0:T(2,128)}) custom-call(f32[3200,128]{1,0:T(8,128)} %bitcast.64, bf16[512,256]{1,0:T(8,128)(2,1)} %gi.3, bf16[512,256]{1,0:T(8,128)(2,1)} %vi.3, bf16[512,256]{1,0:T(8,128)(2,1)} %og.3, ...), custom_call_target="tpu_custom_call" | custom-call | flops 1572864 | bytes 4194304 | tf_op jit(solution)/shard_map/pallas_call | solution.py:163
  (9 shorter events, 0.1 us)
Async XLA Ops:
  3.2 31.7 %all-to-all-start = ((f32[128,1,2176]{2,1,0:T(1,128)}), f32[128,1,2176]{2,1,0:T(1,128)S(1)}, u32[]{:S(2)}, u32[]{:S(2)}) async-start(f32[128,1,2176]{2,1,0:T(1,128)} %bitcast.74), calls=%async_computation | async-start | bytes 2228224 | tf_op jit(solution)/shard_map/all_to_all | solution.py:66

commit v6 on v5

--- a/solution.py
+++ b/solution.py
@@ -138,39 +138,54 @@
     back = lax.all_to_all(out_send.reshape(dev_n, -1), ("seq", "chan"), 0, 0, tiled=True)
 
     def tail_kernel(bk, gi, vi, og, ot, sg, o_gg, o_gog, o_gv, o_taps, o_skip):
+        f2 = pl.program_id(0)
+
         def field(first):
             parts = [bk[pl.ds(first + q, dev_n, stride=back_w), :] for q in range(rq)]
             return jnp.concatenate(parts, axis=1).T
 
-        for f2 in range(per_dev):
-            lanes = pl.ds(f2 * dev_n, dev_n)
-            conv = field(f2 * rq)
-            corr = field((per_dev + f2) * rq)
-            o_taps[:, lanes] = field((2 * per_dev + f2) * rq)
-            gate = gi[:, lanes].astype(F32)
-            val = vi[:, lanes].astype(F32)
-            outg = og[:, lanes].astype(F32)
-            m = (gate * val).astype(jnp.bfloat16).astype(F32)
-            g = (outg * ot[:, lanes].astype(F32)).astype(jnp.bfloat16).astype(F32)
-            s = sg[:, lanes]
-            o_gog[:, lanes] = (outg * (conv + s * m)).astype(jnp.bfloat16)
-            mix = corr + s * g
-            o_gg[:, lanes] = (mix * val).astype(jnp.bfloat16)
-            o_gv[:, lanes] = (mix * gate).astype(jnp.bfloat16)
-        o_skip[...] = bk[pl.ds(3 * per_dev * rq, dev_n, stride=back_w), :].T[:per_dev, :]
-
+        conv = field(f2 * rq)
+        corr = field((per_dev + f2) * rq)
+        o_taps[...] = field((2 * per_dev + f2) * rq)
+        gate = gi[...].astype(F32)
+        val = vi[...].astype(F32)
+        outg = og[...].astype(F32)
+        m = (gate * val).astype(jnp.bfloat16).astype(F32)
+        g = (outg * ot[...].astype(F32)).astype(jnp.bfloat16).astype(F32)
+        s = sg[...]
+        o_gog[...] = (outg * (conv + s * m)).astype(jnp.bfloat16)
+        mix = corr + s * g
+        o_gg[...] = (mix * val).astype(jnp.bfloat16)
+        o_gv[...] = (mix * gate).astype(jnp.bfloat16)
+
+        @pl.when(f2 == 0)
+        def _():
+            o_skip[...] = bk[pl.ds(3 * per_dev * rq, dev_n, stride=back_w), :].T[:8, :]
+
+    half = pl.BlockSpec((rows, dev_n), lambda f: (0, f))
     grad_shape = jax.ShapeDtypeStruct((rows, local_ch), jnp.bfloat16)
-    grad_gate, grad_out_gate, grad_value, taps_grad, skip_two = pl.pallas_call(
+    grad_gate, grad_out_gate, grad_value, taps_grad, skip_rows = pl.pallas_call(
         tail_kernel,
+        grid=(per_dev,),
+        in_specs=[
+            pl.BlockSpec((dev_n * back_w, lane), lambda f: (0, 0)),
+            half,
+            half,
+            half,
+            half,
+            pl.BlockSpec((1, dev_n), lambda f: (0, f)),
+        ],
+        out_specs=(half, half, half, half, pl.BlockSpec((8, dev_n), lambda f: (0, 0))),
         out_shape=(
             grad_shape,
             grad_shape,
             grad_shape,
             jax.ShapeDtypeStruct((rows, filters), F32),
-            jax.ShapeDtypeStruct((per_dev, dev_n), F32),
+            jax.ShapeDtypeStruct((8, dev_n), F32),
         ),
         cost_estimate=pl.CostEstimate(flops=12 * rows * local_ch, transcendentals=0, bytes_accessed=4 * 4 * rows * local_ch * 2),
     )(back.reshape(dev_n * back_w, lane), gate_in, value_in, out_grad, out_gate, skip_gain.reshape(1, local_ch))
+    skip_two = skip_rows[:per_dev]
     skip_grad = skip_two.reshape(local_ch)
     return (grad_gate, grad_out_gate, grad_value, skip_grad, taps_grad)
 

time: 77.5 us -> 79 us (1.019)
  local copies, waits for them, and re-layouts: 2.92 us -> 4.16 us
    reshape x0 -> x1, local copies, waits for them, and re-layouts: none -> 1.24 us  [body(): skip_grad = skip_two.reshape(local_ch)]
where the time goes in v6:
time: 79 us; the launch traced here: 78.7 us
  blocking collectives  29.5 us (37%)
  waiting for transfers between devices  19.5 us (25%)
  starting transfers between devices  11.5 us (15%)
  Pallas kernels  5.93 us (8%)
  matrix products  5.84 us (7%)
  local copies, waits for them, and re-layouts  4.16 us (5%)
  other arithmetic  1.44 us (2%)
  between operations  0.86 us (1%)
    all_to_all x1, blocking collectives, body(): lax.all_to_all(out_send.reshape(dev_n, -1), ('seq', 'chan'), 0, 0, tiled=...  29.5 us
    all_to_all x1, waiting for transfers between devices, body(): lax.all_to_all(send, ('seq', 'chan'), 0, 0, tiled=True)  19.5 us
    all_to_all x1, starting transfers between devices, body(): lax.all_to_all(send, ('seq', 'chan'), 0, 0, tiled=True)  11.5 us
    dot_general x6, matrix products, mm(): return jnp.einsum(spec, a, b, precision=HIGH, preferred_element_type=F32)  5.84 us
    pallas_call x1, Pallas kernels, body(): pl.pallas_call(tail_kernel, grid=(per_dev,), in_specs=[pl.BlockSpec((dev_...  3.33 us
    pallas_call x1, Pallas kernels, body(): pl.pallas_call(prep_kernel, out_shape=jax.ShapeDtypeStruct((dev_n * send_...  2.6 us
  transfers between devices with their start and end apart: 1, of which 1 were waited for; matrix products, arithmetic and copies ran while one was open for 1% of the time, Pallas kernels for 0%

profile of v6, /device:TPU:1, one launch (start us, length us, event | category | flops | bytes accessed | tf_op | source)
XLA Modules:
  0.0 78.7 jit_solution(7657152891991297145)
XLA Ops:
  0.6 2.6 %shard_map.101 = f32[2176,128]{1,0:T(8,128)} custom-call(bf16[512,256]{1,0:T(8,128)(2,1)} %gi.3, bf16[512,256]{1,0:T(8,128)(2,1)} %vi.3, bf16[512,256]{1,0:T(8,128)(2,1)} %og.3, bf16[512,256]{1,0:T(8,128)(2,1)} %ot.3, f32[512,256]{1,0:T(8,128)} %ft.1), custom_call_target="tpu_custom_call" | custom-call | flops 524288 | bytes 2097152 | tf_op jit(solution)/shard_map/pallas_call | solution.py:61
  3.2 11.5 %all-to-all-start = ((f32[128,1,2176]{2,1,0:T(1,128)}), f32[128,1,2176]{2,1,0:T(1,128)S(1)}, u32[]{:S(2)}, u32[]{:S(2)}) async-start(f32[128,1,2176]{2,1,0:T(1,128)} %bitcast.75), calls=%async_computation | async-start | bytes 2228224 | tf_op jit(solution)/shard_map/all_to_all | solution.py:66
  14.7 0.3 fusion.78
  15.0 0.2 fusion.79
  15.2 0.3 fusion.65
  15.4 19.5 %all-to-all-done = f32[128,1,2176]{2,1,0:T(1,128)S(1)} async-done(((f32[128,1,2176]{2,1,0:T(1,128)}), f32[128,1,2176]{2,1,0:T(1,128)S(1)}, u32[]{:S(2)}, u32[]{:S(2)}) %all-to-all-start) | async-done | bytes 1114144 | tf_op jit(solution)/shard_map/all_to_all | solution.py:66
  34.9 0.1 copy.39
  35.0 0.1 fusion.109
  35.1 0.1 copy.30
  35.3 0.2 multiply_reduce_fusion
  35.4 0.1 copy.29
  35.6 0.1 reshape_squeeze.3
  35.7 0.1 copy.31
  35.8 0.1 reshape.122
  35.9 0.8 %fusion.26 = f32[65,34,128]{2,0,1:T(8,128)S(1)} fusion(f32[64,2,128]{2,0,1:T(8,128)S(1)} %reshape.122, f32[64,16,128]{2,0,1:T(8,128)S(1)} %bitcast.66, f32[64,16,128]{2,0,1:T(8,128)S(1)} %bitcast.68), kind=kOutput, calls=%fused_computation.34 | convolution fusion | flops 109241216 | bytes 2245632 | tf_op jit(solution)/shard_map/ks,scr->kcr/dot_general | solution.py:23
  36.8 1.1 %multiply_add_fusion = (f32[65,34,128]{2,0,1:T(8,128)S(1)}, f32[65,34,128]{2,0,1:T(8,128)S(1)}) fusion(f32[65,34,128]{2,0,1:T(8,128)S(1)} %fusion.26, f32[65,128]{1,0:T(8,128)S(1)} %get-tuple-element.27, f32[65,128]{1,0:T(8,128)S(1)} %get-tuple-element.28, f32[64,2,128]{2,0,1:T(8,128)S(1)} %reshape.122, f32[64,16,128]{2,0,1:T(8,128)S(1)} %bitcast.67, ...), kind=kOutput, calls=%fused_computation.24 | convolution fusion | flops 110942656 | bytes 4575232 | tf_op jit(solution)/shard_map/ks,scr->kcr/dot_general | solution.py:23
  37.9 1.2 %fusion = f32[65,34,256]{2,0,1:T(8,128)S(1)} fusion(f32[65,34,128]{2,0,1:T(8,128)S(1)} %get-tuple-element.20, f32[65,34,128]{2,0,1:T(8,128)S(1)} %get-tuple-element.19, f32[128,128]{1,0:T(8,128)S(1)} %get-tuple-element.30, f32[128,128]{1,0:T(8,128)S(1)} %get-tuple-element.29, f32[128,128]{1,0:T(8,128)S(1)} %fusion.78), kind=kOutput, calls=%fused_computation | convolution fusion | flops 869769728 | bytes 4722688 | tf_op jit(solution)/shard_map/kcn,nm->kcm/dot_general | solution.py:23
  39.1 0.1 multiply_add_fusion.1
  39.2 0.1 broadcast_in_dim.18
  39.3 0.2 multiply_subtract_fusion.3
  39.6 1.2 %fusion.4 = f32[65,34,256]{2,0,1:T(8,128)S(1)} fusion(f32[65,2,256]{2,0,1:T(8,128)S(1)} %bitcast_reduce_fusion, f32[65,16,128]{2,0,1:T(8,128)S(1)} %get-tuple-element.17, f32[65,16,128]{2,0,1:T(8,128)S(1)} %get-tuple-element.16, f32[65,16,128]{2,0,1:T(8,128)S(1)} %get-tuple-element.18, f32[65,16,128]{2,0,1:T(8,128)S(1)} %get-tuple-element.15, ...), kind=kOutput, calls=%fused_computation.4 | convolution fusion | flops 871467008 | bytes 4722688 | tf_op jit(solution)/shard_map/kcn,nm->kcm/dot_general | solution.py:23
  40.8 0.8 fusion.17
  41.6 0.8 %convolution_subtract_fusion = f32[64,34,128]{2,0,1:T(8,128)S(1)} fusion(f32[64,34,128]{2,0,1:T(8,128)S(1)} %fusion.17, f32[65,34,256]{2,0,1:T(8,128)S(1)} %fusion.4, f32[65,128]{1,0:T(8,128)S(1)} %get-tuple-element.27, f32[65,128]{1,0:T(8,128)S(1)} %get-tuple-element.28, f32[65]{0:T(128)S(1)} %fusion.87), kind=kOutput, calls=%fused_computation.15 | convolution fusion | flops 109815488 | bytes 4558084 | tf_op jit(solution)/shard_map/ik,kcr->icr/dot_general | solution.py:23
  42.4 0.1 fusion.108
  42.5 0.1 copy.36
  42.6 0.3 copy.32
  42.9 0.3 copy.33
  43.3 0.1 pad_maximum_fusion
  43.5 1.1 %all_to_all.14 = f32[128,1,3200]{2,1,0:T(1,128)S(1)} reshape(f32[128,3200]{1,0:T(8,128)S(1)} %pad_maximum_fusion) | data formatting | bytes 3276800 | tf_op jit(solution)/shard_map/all_to_all | solution.py:138
  44.6 29.5 %all_to_all.18 = f32[128,1,3200]{2,1,0:T(1,128)} all-to-all(f32[128,1,3200]{2,1,0:T(1,128)S(1)} %all_to_all.14), channel_id=1, replica_groups=mesh['seq'=16,'chan'=8] {'seq','chan'}, dimensions={0} | all-to-all | bytes 3276800 | tf_op jit(solution)/shard_map/all_to_all | solution.py:138
  74.1 3.3 %shard_map.102 = (bf16[512,256]{1,0:T(8,128)(2,1)}, bf16[512,256]{1,0:T(8,128)(2,1)}, bf16[512,256]{1,0:T(8,128)(2,1)}, f32[512,256]{1,0:T(8,128)}, f32[8,128]{1,0:T(8,128)}) custom-call(f32[3200,128]{1,0:T(8,128)} %bitcast.65, bf16[512,256]{1,0:T(8,128)(2,1)} %gi.3, bf16[512,256]{1,0:T(8,128)(2,1)} %vi.3, bf16[512,256]{1,0:T(8,128)(2,1)} %og.3, ...), custom_call_target="tpu_custom_call" | custom-call | flops 1572864 | bytes 4194304 | tf_op jit(solution)/shard_map/pallas_call | solution.py:167
  77.4 1.2 %slice_bitcast_fusion = f32[256]{0:T(256)} fusion(f32[8,128]{1,0:T(8,128)} %get-tuple-element.13), kind=kLoop, calls=%fused_computation.116 | loop fusion | bytes 2048 | tf_op jit(solution)/shard_map/reshape | solution.py:189
  (10 shorter events, 0.2 us)
Async XLA Ops:
  3.2 31.7 %all-to-all-start = ((f32[128,1,2176]{2,1,0:T(1,128)}), f32[128,1,2176]{2,1,0:T(1,128)S(1)}, u32[]{:S(2)}, u32[]{:S(2)}) async-start(f32[128,1,2176]{2,1,0:T(1,128)} %bitcast.75), calls=%async_computation | async-start | bytes 2228224 | tf_op jit(solution)/shard_map/all_to_all | solution.py:66

commit v7 on v5

--- a/solution.py
+++ b/solution.py
@@ -82,7 +82,11 @@
     h_pos = h_pos.transpose(0, 1, 3, 2, 4).reshape(blocks, per_dev, lane)
     skip_mine = jnp.sum(m_pos * g_pos, axis=(0, 2)).reshape(per_dev, chan_n).T
 
+    k1_true = k1
+    k1 = -(-k1_true // 8) * 8
+    live = (lax.iota(jnp.int32, k1) < k1_true).astype(F32)[:, None]
     c1, s1 = trig(k1, blocks, 2 * blocks)
+    w1 = jnp.concatenate([c1 * live, -s1 * live], axis=0)
     tw_c, tw_s = trig(k1, lane, length)
     tw_c = tw_c[:, None, :]
     tw_s = tw_s[:, None, :]
@@ -93,16 +97,15 @@
     w_inv = jnp.concatenate(
         [jnp.concatenate([c2, s2], axis=1), jnp.concatenate([-s2, c2], axis=1)], axis=0
     )
-    weight = jnp.where(
-        (lax.iota(jnp.int32, k1) == 0) | (lax.iota(jnp.int32, k1) == blocks), 1.0, 2.0
-    ) / length
+    rows_k = lax.iota(jnp.int32, k1)
+    weight = jnp.where((rows_k == 0) | (rows_k == blocks), 1.0, 2.0)
+    weight = jnp.where(rows_k < k1_true, weight, 0.0) / length
     ci, si = trig(blocks, k1, 2 * blocks)
-    ci = ci * weight[None, :]
-    si = si * weight[None, :]
+    wi = jnp.concatenate([ci * weight[None, :], -si * weight[None, :]], axis=1)
 
     fields = jnp.concatenate([m_pos, g_pos, h_pos], axis=1)
-    are = mm("ks,scr->kcr", c1, fields)
-    aim = mm("ks,scr->kcr", -s1, fields)
+    a = mm("ks,scr->kcr", w1, fields)
+    are, aim = a[:k1], a[k1:]
     turned = jnp.concatenate([are * tw_c + aim * tw_s, aim * tw_c - are * tw_s], axis=2)
     spec = mm("kcn,nm->kcm", turned, w_fwd)
 
@@ -122,7 +125,7 @@
     zre, zim = z[:, :, :lane], z[:, :, lane:]
     ure = zre * tw_c - zim * tw_s
     uim = zre * tw_s + zim * tw_c
-    y = mm("ik,kcr->icr", ci, ure) - mm("ik,kcr->icr", si, uim)
+    y = mm("ik,kcr->icr", wi, jnp.concatenate([ure, uim], axis=0))
 
     def by_chunk(block, copies):
         block = block.reshape(seq_n, qn, per_dev, copies, lane).transpose(0, 3, 2, 1, 4)

time: 77.5 us -> 76.7 us (0.990)
  matrix products: 5.84 us -> 4.62 us
  other arithmetic: 1.44 us -> 2.27 us
    dot_general x6 -> x4, matrix products: 5.84 us -> 4.62 us  [mm(): return jnp.einsum(spec, a, b, precision=HIGH, preferred_element_type=F32)]
where the time goes in v7:
time: 76.7 us; the launch traced here: 76.5 us
  blocking collectives  29.5 us (38%)
  waiting for transfers between devices  19.1 us (25%)
  starting transfers between devices  11.5 us (15%)
  Pallas kernels  5.7 us (7%)
  matrix products  4.62 us (6%)
  local copies, waits for them, and re-layouts  2.89 us (4%)
  other arithmetic  2.27 us (3%)
  between operations  0.87 us (1%)
    all_to_all x1, blocking collectives, body(): lax.all_to_all(out_send.reshape(dev_n, -1), ('seq', 'chan'), 0, 0, tiled=...  29.5 us
    all_to_all x1, waiting for transfers between devices, body(): lax.all_to_all(send, ('seq', 'chan'), 0, 0, tiled=True)  19.1 us
    all_to_all x1, starting transfers between devices, body(): lax.all_to_all(send, ('seq', 'chan'), 0, 0, tiled=True)  11.5 us
    dot_general x4, matrix products, mm(): return jnp.einsum(spec, a, b, precision=HIGH, preferred_element_type=F32)  4.62 us
    pallas_call x1, Pallas kernels, body(): pl.pallas_call(tail_kernel, out_shape=(grad_shape, grad_shape, grad_shape...  3.1 us
    pallas_call x1, Pallas kernels, body(): pl.pallas_call(prep_kernel, out_shape=jax.ShapeDtypeStruct((dev_n * send_...  2.6 us
  transfers between devices with their start and end apart: 1, of which 1 were waited for; matrix products, arithmetic and copies ran while one was open for 1% of the time, Pallas kernels for 0%

profile of v7, /device:TPU:1, one launch (start us, length us, event | category | flops | bytes accessed | tf_op | source)
XLA Modules:
  0.0 76.5 jit_solution(5959566344015136547)
XLA Ops:
  0.6 2.6 %shard_map.101 = f32[2176,128]{1,0:T(8,128)} custom-call(bf16[512,256]{1,0:T(8,128)(2,1)} %gi.3, bf16[512,256]{1,0:T(8,128)(2,1)} %vi.3, bf16[512,256]{1,0:T(8,128)(2,1)} %og.3, bf16[512,256]{1,0:T(8,128)(2,1)} %ot.3, f32[512,256]{1,0:T(8,128)} %ft.1), custom_call_target="tpu_custom_call" | custom-call | flops 524288 | bytes 2097152 | tf_op jit(solution)/shard_map/pallas_call | solution.py:61
  3.2 11.5 %all-to-all-start = ((f32[128,1,2176]{2,1,0:T(1,128)}), f32[128,1,2176]{2,1,0:T(1,128)S(1)}, u32[]{:S(2)}, u32[]{:S(2)}) async-start(f32[128,1,2176]{2,1,0:T(1,128)} %bitcast.62), calls=%async_computation | async-start | bytes 2228224 | tf_op jit(solution)/shard_map/all_to_all | solution.py:66
  14.7 0.3 fusion.64
  15.0 0.2 fusion.65
  15.2 0.3 fusion.56
  15.5 0.2 cosine_multiply_fusion
  15.6 0.2 cosine_multiply_fusion.1
  15.8 19.1 %all-to-all-done = f32[128,1,2176]{2,1,0:T(1,128)S(1)} async-done(((f32[128,1,2176]{2,1,0:T(1,128)}), f32[128,1,2176]{2,1,0:T(1,128)S(1)}, u32[]{:S(2)}, u32[]{:S(2)}) %all-to-all-start) | async-done | bytes 1114144 | tf_op jit(solution)/shard_map/all_to_all | solution.py:66
  34.9 0.1 copy.39
  35.0 0.1 fusion.73
  35.1 0.1 copy.30
  35.3 0.2 multiply_reduce_fusion
  35.4 0.1 copy.29
  35.6 0.1 reshape_squeeze.3
  35.8 0.1 reshape.128
  35.9 1.2 %fusion.18 = f32[144,34,128]{2,0,1:T(8,128)S(1)} fusion(f32[64,2,128]{2,0,1:T(8,128)S(1)} %reshape.128, f32[64,16,128]{2,0,1:T(8,128)S(1)} %bitcast.65, f32[64,16,128]{2,0,1:T(8,128)S(1)} %bitcast.66, f32[72,64]{0,1:T(8,128)S(1)} %get-tuple-element.32, f32[72,64]{0,1:T(8,128)S(1)} %get-tuple-element.31), kind=kOutput, calls=%fused_computation.25 | convolution fusion | flops 241214464 | bytes 3657728 | tf_op jit(solution)/shard_map/ks,scr->kcr/dot_general | solution.py:23
  37.2 0.3 multiply_add_fusion.1
  37.4 1.2 %fusion = f32[72,34,256]{2,0,1:T(8,128)S(1)} fusion(f32[72,34,128]{2,0,1:T(8,128)S(1)} %get-tuple-element.22, f32[72,34,128]{2,0,1:T(8,128)S(1)} %get-tuple-element.21, f32[128,128]{1,0:T(8,128)S(1)} %get-tuple-element.36, f32[128,128]{1,0:T(8,128)S(1)} %get-tuple-element.35, f32[128,128]{1,0:T(8,128)S(1)} %fusion.64), kind=kOutput, calls=%fused_computation | convolution fusion | flops 963416064 | bytes 5210112 | tf_op jit(solution)/shard_map/kcn,nm->kcm/dot_general | solution.py:23
  38.7 0.1 multiply_add_fusion.2
  38.8 0.1 broadcast_in_dim.23
  38.9 0.2 multiply_subtract_fusion.4
  39.2 1.2 %fusion.4 = f32[72,34,256]{2,0,1:T(8,128)S(1)} fusion(f32[72,2,256]{2,0,1:T(8,128)S(1)} %bitcast_reduce_fusion, f32[72,16,128]{2,0,1:T(8,128)S(1)} %get-tuple-element.17, f32[72,16,128]{2,0,1:T(8,128)S(1)} %get-tuple-element.16, f32[72,16,128]{2,0,1:T(8,128)S(1)} %get-tuple-element.18, f32[72,16,128]{2,0,1:T(8,128)S(1)} %get-tuple-element.15, ...), kind=kOutput, calls=%fused_computation.4 | convolution fusion | flops 965296128 | bytes 5210112 | tf_op jit(solution)/shard_map/kcn,nm->kcm/dot_general | solution.py:23
  40.4 0.3 multiply_subtract_fusion
  40.7 1.0 %fusion.14 = f32[64,34,128]{2,0,1:T(8,128)S(1)} fusion(f32[72,34,128]{2,0,1:T(8,128)S(1)} %get-tuple-element.20, f32[72,34,128]{2,0,1:T(8,128)S(1)} %get-tuple-element.19, f32[64,72]{1,0:T(8,128)S(1)} %get-tuple-element.30, f32[64,72]{1,0:T(8,128)S(1)} %get-tuple-element.29), kind=kOutput, calls=%fused_computation.14 | convolution fusion | flops 241284096 | bytes 3657728 | tf_op jit(solution)/shard_map/ik,kcr->icr/dot_general | solution.py:23
  41.7 0.1 fusion.72
  41.8 0.1 copy.36
  41.9 0.3 copy.32
  42.2 0.3 copy.33
  42.6 0.1 pad_maximum_fusion
  42.7 1.1 %all_to_all.14 = f32[128,1,3200]{2,1,0:T(1,128)S(1)} reshape(f32[128,3200]{1,0:T(8,128)S(1)} %pad_maximum_fusion) | data formatting | bytes 3276800 | tf_op jit(solution)/shard_map/all_to_all | solution.py:141
  43.9 29.5 %all_to_all.18 = f32[128,1,3200]{2,1,0:T(1,128)} all-to-all(f32[128,1,3200]{2,1,0:T(1,128)S(1)} %all_to_all.14), channel_id=1, replica_groups=mesh['seq'=16,'chan'=8] {'seq','chan'}, dimensions={0} | all-to-all | bytes 3276800 | tf_op jit(solution)/shard_map/all_to_all | solution.py:141
  73.4 3.1 %shard_map.102 = (bf16[512,256]{1,0:T(8,128)(2,1)}, bf16[512,256]{1,0:T(8,128)(2,1)}, bf16[512,256]{1,0:T(8,128)(2,1)}, f32[512,256]{1,0:T(8,128)}, f32[2,128]{1,0:T(2,128)}) custom-call(f32[3200,128]{1,0:T(8,128)} %bitcast.56, bf16[512,256]{1,0:T(8,128)(2,1)} %gi.3, bf16[512,256]{1,0:T(8,128)(2,1)} %vi.3, bf16[512,256]{1,0:T(8,128)(2,1)} %og.3, ...), custom_call_target="tpu_custom_call" | custom-call | flops 1572864 | bytes 4194304 | tf_op jit(solution)/shard_map/pallas_call | solution.py:166
  (12 shorter events, 0.3 us)
Async XLA Ops:
  3.2 31.7 %all-to-all-start = ((f32[128,1,2176]{2,1,0:T(1,128)}), f32[128,1,2176]{2,1,0:T(1,128)S(1)}, u32[]{:S(2)}, u32[]{:S(2)}) async-start(f32[128,1,2176]{2,1,0:T(1,128)} %bitcast.62), calls=%async_computation | async-start | bytes 2228224 | tf_op jit(solution)/shard_map/all_to_all | solution.py:66

commit v8 on v7

--- a/solution.py
+++ b/solution.py
@@ -44,7 +44,10 @@
     back_w = (3 * span + pad_w) // lane
     rq = rows // lane
 
-    def prep_kernel(gi, vi, og, ot, ft, send):
+    def prep_kernel(gi, vi, og, ot, ft, send, taps_buf, taps_sem):
+        first = pl.multiple_of(lax.axis_index("chan") * part, part)
+        taps_copy = pltpu.make_async_copy(ft.at[pl.ds(first, part), :], taps_buf, taps_sem)
+        taps_copy.start()
         for f2 in range(per_dev):
             lanes = pl.ds(f2 * dev_n, dev_n)
             m = (gi[:, lanes].astype(F32) * vi[:, lanes].astype(F32)).astype(jnp.bfloat16).astype(F32).T
@@ -52,15 +55,18 @@
             for q in range(rq):
                 send[pl.ds(f2 * rq + q, dev_n, stride=send_w), :] = m[:, q * lane : (q + 1) * lane]
                 send[pl.ds((per_dev + f2) * rq + q, dev_n, stride=send_w), :] = g[:, q * lane : (q + 1) * lane]
-        first = pl.multiple_of(lax.axis_index("chan") * part, part)
+        taps_copy.wait()
         window = jnp.concatenate(
-            [ft[pl.ds(first, part), pl.ds(f2 * dev_n, dev_n)] for f2 in range(per_dev)], axis=0
+            [taps_buf[:, pl.ds(f2 * dev_n, dev_n)] for f2 in range(per_dev)], axis=0
         )
         send[pl.ds(2 * per_dev * rq, dev_n, stride=send_w), :] = window.T
 
     send = pl.pallas_call(
         prep_kernel,
         out_shape=jax.ShapeDtypeStruct((dev_n * send_w, lane), F32),
+        in_specs=[pl.BlockSpec(memory_space=pltpu.VMEM)] * 4 + [pl.BlockSpec(memory_space=pl.ANY)],
+        out_specs=pl.BlockSpec(memory_space=pltpu.VMEM),
+        scratch_shapes=[pltpu.VMEM((part, filters), F32), pltpu.SemaphoreType.DMA(())],
         cost_estimate=pl.CostEstimate(flops=4 * rows * local_ch, transcendentals=0, bytes_accessed=4 * 2 * rows * local_ch * 2),
     )(gate_in, value_in, out_grad, out_gate, filter_taps).reshape(dev_n, send_w * lane)
     recv = lax.all_to_all(send, ("seq", "chan"), 0, 0, tiled=True).reshape(seq_n, chan_n, -1)

time: 76.7 us -> 77.3 us (level)
  no operation moved by 1% of the time
where the time goes in v8:
time: 77.3 us; the launch traced here: 77 us
  blocking collectives  29.5 us (38%)
  waiting for transfers between devices  19.1 us (25%)
  starting transfers between devices  11.5 us (15%)
  Pallas kernels  6.24 us (8%)
  matrix products  4.62 us (6%)
  local copies, waits for them, and re-layouts  2.89 us (4%)
  other arithmetic  2.27 us (3%)
  between operations  0.87 us (1%)
    all_to_all x1, blocking collectives, body(): lax.all_to_all(out_send.reshape(dev_n, -1), ('seq', 'chan'), 0, 0, tiled=...  29.5 us
    all_to_all x1, waiting for transfers between devices, body(): lax.all_to_all(send, ('seq', 'chan'), 0, 0, tiled=True)  19.1 us
    all_to_all x1, starting transfers between devices, body(): lax.all_to_all(send, ('seq', 'chan'), 0, 0, tiled=True)  11.5 us
    dot_general x4, matrix products, mm(): return jnp.einsum(spec, a, b, precision=HIGH, preferred_element_type=F32)  4.62 us
    pallas_call x1, Pallas kernels, body(): pl.pallas_call(prep_kernel, out_shape=jax.ShapeDtypeStruct((dev_n * send_...  3.14 us
    pallas_call x1, Pallas kernels, body(): pl.pallas_call(tail_kernel, out_shape=(grad_shape, grad_shape, grad_shape...  3.1 us
  transfers between devices with their start and end apart: 1, of which 1 were waited for; matrix products, arithmetic and copies ran while one was open for 1% of the time, Pallas kernels for 0%

profile of v8, /device:TPU:1, one launch (start us, length us, event | category | flops | bytes accessed | tf_op | source)
XLA Modules:
  0.0 77.0 jit_solution(15853427116653139275)
XLA Ops:
  0.6 3.1 %shard_map.101 = f32[2176,128]{1,0:T(8,128)} custom-call(bf16[512,256]{1,0:T(8,128)(2,1)} %gi.3, bf16[512,256]{1,0:T(8,128)(2,1)} %vi.3, bf16[512,256]{1,0:T(8,128)(2,1)} %og.3, bf16[512,256]{1,0:T(8,128)(2,1)} %ot.3, f32[512,256]{1,0:T(8,128)} %ft.1), custom_call_target="tpu_custom_call" | custom-call | flops 524288 | bytes 2097152 | tf_op jit(solution)/shard_map/pallas_call | solution.py:64
  3.8 11.5 %all-to-all-start = ((f32[128,1,2176]{2,1,0:T(1,128)}), f32[128,1,2176]{2,1,0:T(1,128)S(1)}, u32[]{:S(2)}, u32[]{:S(2)}) async-start(f32[128,1,2176]{2,1,0:T(1,128)} %bitcast.62), calls=%async_computation | async-start | bytes 2228224 | tf_op jit(solution)/shard_map/all_to_all | solution.py:72
  15.3 0.3 fusion.64
  15.6 0.2 fusion.65
  15.7 0.3 fusion.56
  16.0 0.2 cosine_multiply_fusion
  16.2 0.2 cosine_multiply_fusion.1
  16.3 19.1 %all-to-all-done = f32[128,1,2176]{2,1,0:T(1,128)S(1)} async-done(((f32[128,1,2176]{2,1,0:T(1,128)}), f32[128,1,2176]{2,1,0:T(1,128)S(1)}, u32[]{:S(2)}, u32[]{:S(2)}) %all-to-all-start) | async-done | bytes 1114144 | tf_op jit(solution)/shard_map/all_to_all | solution.py:72
  35.4 0.1 copy.39
  35.5 0.1 fusion.73
  35.7 0.1 copy.30
  35.8 0.2 multiply_reduce_fusion
  36.0 0.1 copy.29
  36.1 0.1 reshape_squeeze.3
  36.3 0.1 reshape.128
  36.5 1.2 %fusion.18 = f32[144,34,128]{2,0,1:T(8,128)S(1)} fusion(f32[64,2,128]{2,0,1:T(8,128)S(1)} %reshape.128, f32[64,16,128]{2,0,1:T(8,128)S(1)} %bitcast.65, f32[64,16,128]{2,0,1:T(8,128)S(1)} %bitcast.66, f32[72,64]{0,1:T(8,128)S(1)} %get-tuple-element.32, f32[72,64]{0,1:T(8,128)S(1)} %get-tuple-element.31), kind=kOutput, calls=%fused_computation.25 | convolution fusion | flops 241214464 | bytes 3657728 | tf_op jit(solution)/shard_map/ks,scr->kcr/dot_general | solution.py:23
  37.7 0.3 multiply_add_fusion.1
  38.0 1.2 %fusion = f32[72,34,256]{2,0,1:T(8,128)S(1)} fusion(f32[72,34,128]{2,0,1:T(8,128)S(1)} %get-tuple-element.22, f32[72,34,128]{2,0,1:T(8,128)S(1)} %get-tuple-element.21, f32[128,128]{1,0:T(8,128)S(1)} %get-tuple-element.36, f32[128,128]{1,0:T(8,128)S(1)} %get-tuple-element.35, f32[128,128]{1,0:T(8,128)S(1)} %fusion.64), kind=kOutput, calls=%fused_computation | convolution fusion | flops 963416064 | bytes 5210112 | tf_op jit(solution)/shard_map/kcn,nm->kcm/dot_general | solution.py:23
  39.2 0.1 multiply_add_fusion.2
  39.3 0.1 broadcast_in_dim.23
  39.4 0.2 multiply_subtract_fusion.4
  39.8 1.2 %fusion.4 = f32[72,34,256]{2,0,1:T(8,128)S(1)} fusion(f32[72,2,256]{2,0,1:T(8,128)S(1)} %bitcast_reduce_fusion, f32[72,16,128]{2,0,1:T(8,128)S(1)} %get-tuple-element.17, f32[72,16,128]{2,0,1:T(8,128)S(1)} %get-tuple-element.16, f32[72,16,128]{2,0,1:T(8,128)S(1)} %get-tuple-element.18, f32[72,16,128]{2,0,1:T(8,128)S(1)} %get-tuple-element.15, ...), kind=kOutput, calls=%fused_computation.4 | convolution fusion | flops 965296128 | bytes 5210112 | tf_op jit(solution)/shard_map/kcn,nm->kcm/dot_general | solution.py:23
  41.0 0.3 multiply_subtract_fusion
  41.2 1.0 %fusion.14 = f32[64,34,128]{2,0,1:T(8,128)S(1)} fusion(f32[72,34,128]{2,0,1:T(8,128)S(1)} %get-tuple-element.20, f32[72,34,128]{2,0,1:T(8,128)S(1)} %get-tuple-element.19, f32[64,72]{1,0:T(8,128)S(1)} %get-tuple-element.30, f32[64,72]{1,0:T(8,128)S(1)} %get-tuple-element.29), kind=kOutput, calls=%fused_computation.14 | convolution fusion | flops 241284096 | bytes 3657728 | tf_op jit(solution)/shard_map/ik,kcr->icr/dot_general | solution.py:23
  42.2 0.1 fusion.72
  42.3 0.1 copy.36
  42.4 0.3 copy.32
  42.7 0.3 copy.33
  43.2 0.1 pad_maximum_fusion
  43.3 1.1 %all_to_all.14 = f32[128,1,3200]{2,1,0:T(1,128)S(1)} reshape(f32[128,3200]{1,0:T(8,128)S(1)} %pad_maximum_fusion) | data formatting | bytes 3276800 | tf_op jit(solution)/shard_map/all_to_all | solution.py:147
  44.4 29.5 %all_to_all.18 = f32[128,1,3200]{2,1,0:T(1,128)} all-to-all(f32[128,1,3200]{2,1,0:T(1,128)S(1)} %all_to_all.14), channel_id=1, replica_groups=mesh['seq'=16,'chan'=8] {'seq','chan'}, dimensions={0} | all-to-all | bytes 3276800 | tf_op jit(solution)/shard_map/all_to_all | solution.py:147
  73.9 3.1 %shard_map.102 = (bf16[512,256]{1,0:T(8,128)(2,1)}, bf16[512,256]{1,0:T(8,128)(2,1)}, bf16[512,256]{1,0:T(8,128)(2,1)}, f32[512,256]{1,0:T(8,128)}, f32[2,128]{1,0:T(2,128)}) custom-call(f32[3200,128]{1,0:T(8,128)} %bitcast.56, bf16[512,256]{1,0:T(8,128)(2,1)} %gi.3, bf16[512,256]{1,0:T(8,128)(2,1)} %vi.3, bf16[512,256]{1,0:T(8,128)(2,1)} %og.3, ...), custom_call_target="tpu_custom_call" | custom-call | flops 1572864 | bytes 4194304 | tf_op jit(solution)/shard_map/pallas_call | solution.py:172
  (12 shorter events, 0.3 us)
Async XLA Ops:
  3.8 31.7 %all-to-all-start = ((f32[128,1,2176]{2,1,0:T(1,128)}), f32[128,1,2176]{2,1,0:T(1,128)S(1)}, u32[]{:S(2)}, u32[]{:S(2)}) async-start(f32[128,1,2176]{2,1,0:T(1,128)} %bitcast.62), calls=%async_computation | async-start | bytes 2228224 | tf_op jit(solution)/shard_map/all_to_all | solution.py:72
